TPU v7x, 512 devices: a whole 4x8x8 slice. The times are simulated.
512 devices in a mesh: lon: 64 (over z_hi, y, core), lat: 8 (over z_lo, x).
Axes of the slice: x: 4, y: 8, z: 8 (z_hi: 4, z_lo: 2; z = z_hi * 2 + z_lo), core: 2. Of those that a mesh axis runs over, the one named last changes fastest.
Arguments:
- concentration: float32 [512, 1792, 128], P('lon', 'lat'), may hold values from -6 to 6
- wind: bfloat16 [3, 512, 1792, 128], P(None, 'lon', 'lat'), may hold values from -0.099609375 to 0.099609375
- kappa: bfloat16 [512, 1792, 128], P('lon', 'lat'), may hold values from 0.0099487305 to 0.059814453
- observed: bfloat16 [512, 1792, 128], P('lon', 'lat'), may hold values from -6 to 6
Outputs:
- grad_conc: float32 [512, 1792, 128], P('lon', 'lat')
- grad_kappa: float32 [512, 1792, 128], P('lon', 'lat')
All inputs are finite; a program needn't handle non-finite values.
Results may differ from a plain program's by a relative error of at most 0.0023.
Values may be sent and summed in bfloat16 or wider, within the bound.
No kernel may reach another device: no remote copies, remote signals or barrier semaphores. Data moves between devices by JAX's collectives and lax.ppermute only.
A program may use at most 128 MiB of HBM per device.

v0:
```python
import functools

import jax
import jax.numpy as jnp
from jax import lax
from jax.experimental import pallas as pl
from jax.experimental.pallas import tpu as pltpu
from jax.sharding import PartitionSpec as P

HALO = 4
PAD = 8


def passed_along(value, axis, steps, periodic):
    count = lax.axis_size(axis)
    if periodic:
        pairs = [(source, (source + steps) % count) for source in range(count)]
    else:
        pairs = [(source, source + steps) for source in range(count) if 0 <= source + steps < count]
    return lax.ppermute(value, axis, pairs)


def pack_kernel(west_rows, east_rows, conc, wind, kappa, observed, to_west, to_east, lows, highs):
    fields = [conc, wind.at[0], wind.at[1], wind.at[2], kappa, observed]
    size = conc.shape[0]
    lats = conc.shape[1]
    for out, rows, first in ((to_west, east_rows, True), (to_east, west_rows, False)):
        part = conc[0:rows[0]] if first else conc[size - rows[0]:size]
        high = part.astype(jnp.bfloat16)
        out[0:rows[0]] = high
        out[rows[0]:2 * rows[0]] = (part - high.astype(jnp.float32)).astype(jnp.bfloat16)
        at = 2 * rows[0]
        for f, r in zip(fields[1:], rows[1:]):
            out[at:at + r] = f[0:r] if first else f[size - r:size]
            at += r
    for n, f in enumerate(fields):
        lows[n] = f[:, 0:HALO].astype(jnp.float32)
        highs[n] = f[:, lats - HALO:lats].astype(jnp.float32)


def lat_halo(lows, highs, block):
    from_south = passed_along(highs, "lat", 1, False)
    from_north = passed_along(lows, "lat", -1, False)
    both = jnp.stack([from_south, from_north])
    west = passed_along(both[:, :, block - HALO:], "lon", 1, True)
    east = passed_along(both[:, :, :HALO], "lon", -1, True)
    return [jnp.concatenate([west[n], both[n], east[n]], 1) for n in range(2)]


def stencil_kernel(west_rows, east_rows, conc_in, wind_in, kappa_in, obs_in, west_p, east_p,
                   south_ref, north_halo, north_ref, gc_ref, gk_ref, raw_ref, own_ref, oth_ref, mid_ref, lam2_ref,
                   lam1_ref):
    fields, rows, lats, levels = raw_ref.shape
    block = conc_in.shape[0]
    f32 = jnp.float32
    north_open = north_ref[...]
    lo = PAD
    hi = lats - PAD
    gap = jnp.zeros((PAD - HALO, levels), f32)

    def put(f, r, core):
        raw_ref[f, r, lo:hi] = core
        raw_ref[f, r, lo - HALO:lo] = south_ref[f, r]
        raw_ref[f, r, hi:hi + HALO] = north_halo[f, r]
        raw_ref[f, r, :lo - HALO] = gap
        raw_ref[f, r, hi + HALO:] = gap

    def own_row(i, carry):
        put(0, i + HALO, conc_in[i])
        for d in range(3):
            put(1 + d, i + HALO, wind_in[d, i].astype(f32))
        put(4, i + HALO, kappa_in[i].astype(f32))
        put(5, i + HALO, obs_in[i].astype(f32))
        return carry

    lax.fori_loop(0, block, own_row, 0)
    empty = jnp.zeros((hi - lo, levels), f32)
    for r in range(HALO):
        put(0, r, west_p[r].astype(f32) + west_p[HALO + r].astype(f32))
        put(0, HALO + block + r, east_p[r].astype(f32) + east_p[HALO + r].astype(f32))
    at_w = 2 * HALO
    at_e = 2 * HALO
    for f in range(1, fields):
        w = west_rows[f]
        e = east_rows[f]
        for r in range(HALO):
            put(f, r, west_p[at_w + r - (HALO - w)].astype(f32) if r >= HALO - w else empty)
            put(f, HALO + block + r, east_p[at_e + r].astype(f32) if r < e else empty)
        at_w += w
        at_e += e
    conc_ref = raw_ref.at[0]
    obs_ref = raw_ref.at[5]
    upper_open = (lax.broadcasted_iota(jnp.int32, (lats, levels), 1) < levels - 1).astype(f32)

    def next_lat(f):
        return pltpu.roll(f, lats - 1, 0)

    def back_lat(f):
        return pltpu.roll(f, 1, 0)

    def next_lev(f):
        return pltpu.roll(f, levels - 1, 1)

    def back_lev(f):
        return pltpu.roll(f, 1, 1)

    def coef_row(i, carry):
        diffuse = raw_ref[4, i]
        for d, opened in ((0, None), (1, north_open), (2, upper_open)):
            speed = raw_ref[1 + d, i]
            own = jnp.maximum(speed, 0.0) + diffuse
            oth = jnp.minimum(speed, 0.0) - diffuse
            if opened is not None:
                own = own * opened
                oth = oth * opened
            own_ref[d, i] = own
            oth_ref[d, i] = oth
        return carry

    lax.fori_loop(0, rows, coef_row, 0)

    def flux0(src, i):
        return own_ref[0, i] * src[i] + oth_ref[0, i] * src[i + 1]

    def advance(src, dst, lo, hi, minus=None):
        def row(i, west0):
            c = src[i]
            f0 = own_ref[0, i] * c + oth_ref[0, i] * src[i + 1]
            f1 = own_ref[1, i] * c + oth_ref[1, i] * next_lat(c)
            f2 = own_ref[2, i] * c + oth_ref[2, i] * next_lev(c)
            out = c - (f0 + f1 + f2) + (west0 + back_lat(f1) + back_lev(f2))
            if minus is not None:
                out = out - minus[i]
            dst[i] = out
            return f0

        lax.fori_loop(lo, hi, row, flux0(src, lo - 1))

    def part0(src, i):
        return oth_ref[0, i] * (src[i + 1] - src[i])

    def retreat_row(src, i, west0):
        lam = src[i]
        g0 = src[i + 1] - lam
        g1 = next_lat(lam) - lam
        g2 = next_lev(lam) - lam
        p0 = oth_ref[0, i] * g0
        p1 = oth_ref[1, i] * g1
        p2 = oth_ref[2, i] * g2
        gained = own_ref[0, i] * g0 + own_ref[1, i] * g1 + own_ref[2, i] * g2
        return lam + gained + (west0 + back_lat(p1) + back_lev(p2)), p0, (g0, g1, g2)

    def kappa_term(gaps, state, i):
        c = state[i]
        return (
            gaps[0] * (c - state[i + 1])
            + gaps[1] * (c - next_lat(c)) * north_open
            + gaps[2] * (c - next_lev(c)) * upper_open
        )

    h = (rows - gc_ref.shape[0]) // 2
    advance(conc_ref, mid_ref, 1, rows - 1)
    advance(mid_ref, lam2_ref, 2, rows - 2, minus=obs_ref)

    def lam1_row(i, west0):
        out, p0, _ = retreat_row(lam2_ref, i, west0)
        lam1_ref[i] = out
        return p0

    lax.fori_loop(3, rows - 3, lam1_row, part0(lam2_ref, 2))

    def last_row(i, west0):
        out, p0, gaps1 = retreat_row(lam1_ref, i, west0)
        lam = lam2_ref[i]
        gaps2 = (lam2_ref[i + 1] - lam, next_lat(lam) - lam, next_lev(lam) - lam)
        kappa = kappa_term(gaps2, mid_ref, i) + kappa_term(gaps1, conc_ref, i)
        gc_ref[i - h] = out[PAD:lats - PAD]
        gk_ref[i - h] = kappa[PAD:lats - PAD]
        return p0

    lax.fori_loop(h, rows - h, last_row, part0(lam1_ref, h - 1))


def chain(concentration, wind, kappa, observed):
    lon_rows, lat_rows, levels = concentration.shape
    lat_total = lat_rows * lax.axis_size("lat")
    fields = [concentration, wind[0], wind[1], wind[2], kappa, observed]
    west_rows = (4, 4, 3, 3, 4, 2)
    east_rows = (4, 3, 3, 3, 3, 2)
    vmem = pltpu.MemorySpace.VMEM
    pack_rows = lambda rows: 2 * rows[0] + sum(rows[1:])
    lat_type = jax.ShapeDtypeStruct((len(fields), lon_rows, HALO, levels), jnp.float32)
    to_west, to_east, lows, highs = pl.pallas_call(
        functools.partial(pack_kernel, west_rows, east_rows),
        out_shape=(
            jax.ShapeDtypeStruct((pack_rows(east_rows), lat_rows, levels), jnp.bfloat16),
            jax.ShapeDtypeStruct((pack_rows(west_rows), lat_rows, levels), jnp.bfloat16),
            lat_type,
            lat_type,
        ),
        in_specs=[pl.BlockSpec(memory_space=vmem)] * 4,
        out_specs=tuple(pl.BlockSpec(memory_space=vmem) for _ in range(4)),
    )(concentration, wind, kappa, observed)
    got = {"east": passed_along(to_west, "lon", -1, True), "west": passed_along(to_east, "lon", 1, True)}
    south, north = lat_halo(lows, highs, lon_rows)
    ext_rows = lon_rows + 2 * HALO
    ext_lats = lat_rows + 2 * PAD
    lat_place = lax.axis_index("lat") * lat_rows - PAD + lax.broadcasted_iota(jnp.int32, (ext_lats, levels), 0)
    north_open = ((lat_place >= 0) & (lat_place < lat_total - 1)).astype(jnp.float32)
    whole = [concentration, wind, kappa, observed, got["west"], got["east"], south, north, north_open]
    vmem = pltpu.MemorySpace.VMEM
    state = pltpu.VMEM((ext_rows, ext_lats, levels), jnp.float32)
    return pl.pallas_call(
        functools.partial(stencil_kernel, west_rows, east_rows),
        out_shape=(
            jax.ShapeDtypeStruct((lon_rows, lat_rows, levels), jnp.float32),
            jax.ShapeDtypeStruct((lon_rows, lat_rows, levels), jnp.float32),
        ),
        in_specs=[pl.BlockSpec(memory_space=vmem) for _ in whole],
        out_specs=(pl.BlockSpec(memory_space=vmem), pl.BlockSpec(memory_space=vmem)),
        scratch_shapes=[
            pltpu.VMEM((len(fields), ext_rows, ext_lats, levels), jnp.float32),
            pltpu.VMEM((3, ext_rows, ext_lats, levels), jnp.float32),
            pltpu.VMEM((3, ext_rows, ext_lats, levels), jnp.float32),
            state,
            state,
            state,
        ],
        compiler_params=pltpu.CompilerParams(vmem_limit_bytes=60 * 1024 * 1024),
    )(*whole)


def solution(mesh):
    return step(mesh)


def step(mesh):
    return jax.shard_map(
        chain,
        mesh=mesh,
        in_specs=(
            P("lon", "lat", None),
            P(None, "lon", "lat", None),
            P("lon", "lat", None),
            P("lon", "lat", None),
        ),
        out_specs=(P("lon", "lat", None), P("lon", "lat", None)),
        check_vma=False,
    )
```

profile of v0, /device:TPU:6, one launch (start us, length us, event | category | flops | bytes accessed | tf_op | source)
XLA Modules:
  0.0 80.1 jit_solution(7474385839555777185)
XLA Ops:
  0.6 3.5 %shard_map.59 = (bf16[22,224,128]{2,1,0:T(8,128)(2,1)}, bf16[24,224,128]{2,1,0:T(8,128)(2,1)}, f32[6,8,4,128]{3,2,1,0:T(4,128)}, f32[6,8,4,128]{3,2,1,0:T(4,128)}) custom-call(f32[8,224,128]{2,1,0:T(8,128)} %conc_in.1, bf16[3,8,224,128]{3,2,1,0:T(8,128)(2,1)} %wind_in.1, bf16[8,224,128]{2,1,0:T(8,128)(2,1)} %kappa_in.1, bf16[8,224,128]{2,1,0:T(8,128)(2,1)} %obs_in.1), custom_call_target="tpu_custom_call" | custom-call | tf_op jit(solution)/shard_map/pallas_call | solution.py:193
  4.1 1.9 %collective-permute-start = (bf16[24,224,128]{2,1,0:T(8,128)(2,1)}, bf16[24,224,128]{2,1,0:T(8,128)(2,1)S(1)}, u32[]{:S(2)}, u32[]{:S(2)}) collective-permute-start(bf16[24,224,128]{2,1,0:T(8,128)(2,1)} %get-tuple-element.6), channel_id=1, source_target_pairs={{0,8},{8,16},{16,24},{24,32},{32,40},{40,48},{48,56},{56,64},{64,7... | collective-permute-start | bytes 4128776 | tf_op jit(solution)/shard_map/ppermute | solution.py:20
  6.0 13.3 %collective-permute-start.1 = (bf16[22,224,128]{2,1,0:T(8,128)(2,1)}, bf16[22,224,128]{2,1,0:T(8,128)(2,1)S(1)}, u32[]{:S(2)}, u32[]{:S(2)}) collective-permute-start(bf16[22,224,128]{2,1,0:T(8,128)(2,1)} %get-tuple-element.7), channel_id=1, source_target_pairs={{0,504},{8,0},{16,8},{24,16},{32,24},{40,32},{48,40},{56,48},{64,5... | collective-permute-start | bytes 3784712 | tf_op jit(solution)/shard_map/ppermute | solution.py:20
  19.3 3.3 %collective-permute-start.2 = (f32[6,8,4,128]{3,2,1,0:T(4,128)}, f32[6,8,4,128]{3,2,1,0:T(4,128)S(1)}, u32[]{:S(2)}, u32[]{:S(2)}) collective-permute-start(f32[6,8,4,128]{3,2,1,0:T(4,128)} %get-tuple-element.8), channel_id=1, source_target_pairs={{0,1},{1,2},{2,3},{3,4},{4,5},{5,6},{6,7},{8,9},{9,10},{10,11},{11... | collective-permute-start | bytes 294920 | tf_op jit(solution)/shard_map/ppermute | solution.py:20
  22.6 2.5 %collective-permute-start.3 = (f32[6,8,4,128]{3,2,1,0:T(4,128)}, f32[6,8,4,128]{3,2,1,0:T(4,128)S(1)}, u32[]{:S(2)}, u32[]{:S(2)}) collective-permute-start(f32[6,8,4,128]{3,2,1,0:T(4,128)} %get-tuple-element.9), channel_id=1, source_target_pairs={{1,0},{2,1},{3,2},{4,3},{5,4},{6,5},{7,6},{9,8},{10,9},{11,10},{12... | collective-permute-start | bytes 294920 | tf_op jit(solution)/shard_map/ppermute | solution.py:20
  25.2 18.4 %collective-permute-done.2 = f32[6,8,4,128]{3,2,1,0:T(4,128)S(1)} collective-permute-done((f32[6,8,4,128]{3,2,1,0:T(4,128)}, f32[6,8,4,128]{3,2,1,0:T(4,128)S(1)}, u32[]{:S(2)}, u32[]{:S(2)}) %collective-permute-start.2) | collective-permute-done | bytes 98336 | tf_op jit(solution)/shard_map/ppermute | solution.py:20
  43.6 0.0 collective-permute-done.3
  43.6 1.9 %collective-permute-start.4 = (f32[2,6,4,4,128]{4,3,2,1,0:T(4,128)S(1)}, f32[2,6,4,4,128]{4,3,2,1,0:T(4,128)S(1)}, u32[]{:S(2)}, u32[]{:S(2)}) collective-permute-start(f32[2,6,4,4,128]{4,3,2,1,0:T(4,128)S(1)} %get-tuple-element.10), channel_id=1, source_target_pairs={{0,8},{8,16},{16,24},{24,32},{32,40},{40,48},{48,56},{56,64},{64,7... | collective-permute-start | bytes 294920 | tf_op jit(solution)/shard_map/ppermute | solution.py:20
  45.6 15.1 %collective-permute-start.5 = (f32[2,6,4,4,128]{4,3,2,1,0:T(4,128)S(1)}, f32[2,6,4,4,128]{4,3,2,1,0:T(4,128)S(1)}, u32[]{:S(2)}, u32[]{:S(2)}) collective-permute-start(f32[2,6,4,4,128]{4,3,2,1,0:T(4,128)S(1)} %get-tuple-element.11), channel_id=1, source_target_pairs={{0,504},{8,0},{16,8},{24,16},{32,24},{40,32},{48,40},{56,48},{64,5... | collective-permute-start | bytes 294920 | tf_op jit(solution)/shard_map/ppermute | solution.py:20
  60.7 0.3 collective-permute-done.4
  61.0 1.8 %collective-permute-done.5 = f32[2,6,4,4,128]{4,3,2,1,0:T(4,128)S(1)} collective-permute-done((f32[2,6,4,4,128]{4,3,2,1,0:T(4,128)S(1)}, f32[2,6,4,4,128]{4,3,2,1,0:T(4,128)S(1)}, u32[]{:S(2)}, u32[]{:S(2)}) %collective-permute-start.5) | collective-permute-done | bytes 98336 | tf_op jit(solution)/shard_map/ppermute | solution.py:20
  62.9 0.9 %pad_maximum_fusion = (f32[6,16,4,128]{3,2,1,0:T(4,128)}, f32[6,16,4,128]{3,2,1,0:T(4,128)}) fusion(f32[6,4,4,128]{3,2,1,0:T(4,128)S(1)} %get-tuple-element.15, f32[6,8,4,128]{3,2,1,0:T(4,128)S(1)} %collective-permute-done.2, f32[6,4,4,128]{3,2,1,0:T(4,128)S(1)} %get-tuple-element.13, f32[6,4,4,128]{3,2,1,0:T(4,128)S(1)} %get-tuple-element.14, ...), kind=kLoop, calls=%fused_computation.2 | loop fusion | flops 196608 | bytes 786432 | tf_op jit(solution)/shard_map/concatenate | solution.py:47
  63.7 0.0 collective-permute-done.1.east_p
  63.8 0.0 copy-start.1
  63.8 0.0 collective-permute-done.west_p
  63.8 0.0 copy-start
  63.8 0.9 %iota.7.north_ref = f32[240,128]{1,0:T(8,128)} broadcast(f32[240]{0:T(256)S(1)} %and_convert_fusion), dimensions={0} | broadcast | bytes 123840 | tf_op jit(solution)/shard_map/iota | solution.py:208
  64.6 0.2 copy-done.1
  64.8 0.5 copy-done
  65.3 14.9 %shard_map.60 = (f32[8,224,128]{2,1,0:T(8,128)}, f32[8,224,128]{2,1,0:T(8,128)}) custom-call(f32[8,224,128]{2,1,0:T(8,128)} %conc_in.1, bf16[3,8,224,128]{3,2,1,0:T(8,128)(2,1)} %wind_in.1, bf16[8,224,128]{2,1,0:T(8,128)(2,1)} %kappa_in.1, bf16[8,224,128]{2,1,0:T(8,128)(2,1)} %obs_in.1, bf16[24,224,128]{2,1,0:T(8,128)(2,1)} %copy-done, ...), custom_call_target="tpu_custom_call" | custom-call | tf_op jit(solution)/shard_map/pallas_call | solution.py:213
  (4 shorter events, 0.1 us)
Async XLA Ops:
  4.1 59.6 %collective-permute-start = (bf16[24,224,128]{2,1,0:T(8,128)(2,1)}, bf16[24,224,128]{2,1,0:T(8,128)(2,1)S(1)}, u32[]{:S(2)}, u32[]{:S(2)}) collective-permute-start(bf16[24,224,128]{2,1,0:T(8,128)(2,1)} %get-tuple-element.6), channel_id=1, source_target_pairs={{0,8},{8,16},{16,24},{24,32},{32,40},{40,48},{48,56},{56,64},{64,7... | collective-permute-start | bytes 4128776 | tf_op jit(solution)/shard_map/ppermute | solution.py:20
  6.0 57.7 %collective-permute-start.1 = (bf16[22,224,128]{2,1,0:T(8,128)(2,1)}, bf16[22,224,128]{2,1,0:T(8,128)(2,1)S(1)}, u32[]{:S(2)}, u32[]{:S(2)}) collective-permute-start(bf16[22,224,128]{2,1,0:T(8,128)(2,1)} %get-tuple-element.7), channel_id=1, source_target_pairs={{0,504},{8,0},{16,8},{24,16},{32,24},{40,32},{48,40},{56,48},{64,5... | collective-permute-start | bytes 3784712 | tf_op jit(solution)/shard_map/ppermute | solution.py:20
  19.3 24.2 %collective-permute-start.2 = (f32[6,8,4,128]{3,2,1,0:T(4,128)}, f32[6,8,4,128]{3,2,1,0:T(4,128)S(1)}, u32[]{:S(2)}, u32[]{:S(2)}) collective-permute-start(f32[6,8,4,128]{3,2,1,0:T(4,128)} %get-tuple-element.8), channel_id=1, source_target_pairs={{0,1},{1,2},{2,3},{3,4},{4,5},{5,6},{6,7},{8,9},{9,10},{10,11},{11... | collective-permute-start | bytes 294920 | tf_op jit(solution)/shard_map/ppermute | solution.py:20
  22.6 20.9 %collective-permute-start.3 = (f32[6,8,4,128]{3,2,1,0:T(4,128)}, f32[6,8,4,128]{3,2,1,0:T(4,128)S(1)}, u32[]{:S(2)}, u32[]{:S(2)}) collective-permute-start(f32[6,8,4,128]{3,2,1,0:T(4,128)} %get-tuple-element.9), channel_id=1, source_target_pairs={{1,0},{2,1},{3,2},{4,3},{5,4},{6,5},{7,6},{9,8},{10,9},{11,10},{12... | collective-permute-start | bytes 294920 | tf_op jit(solution)/shard_map/ppermute | solution.py:20
  43.6 17.4 %collective-permute-start.4 = (f32[2,6,4,4,128]{4,3,2,1,0:T(4,128)S(1)}, f32[2,6,4,4,128]{4,3,2,1,0:T(4,128)S(1)}, u32[]{:S(2)}, u32[]{:S(2)}) collective-permute-start(f32[2,6,4,4,128]{4,3,2,1,0:T(4,128)S(1)} %get-tuple-element.10), channel_id=1, source_target_pairs={{0,8},{8,16},{16,24},{24,32},{32,40},{40,48},{48,56},{56,64},{64,7... | collective-permute-start | bytes 294920 | tf_op jit(solution)/shard_map/ppermute | solution.py:20
  45.6 17.3 %collective-permute-start.5 = (f32[2,6,4,4,128]{4,3,2,1,0:T(4,128)S(1)}, f32[2,6,4,4,128]{4,3,2,1,0:T(4,128)S(1)}, u32[]{:S(2)}, u32[]{:S(2)}) collective-permute-start(f32[2,6,4,4,128]{4,3,2,1,0:T(4,128)S(1)} %get-tuple-element.11), channel_id=1, source_target_pairs={{0,504},{8,0},{16,8},{24,16},{32,24},{40,32},{48,40},{56,48},{64,5... | collective-permute-start | bytes 294920 | tf_op jit(solution)/shard_map/ppermute | solution.py:20
  63.8 1.1 %copy-start.1 = (bf16[22,224,128]{2,1,0:T(8,128)(2,1)}, bf16[22,224,128]{2,1,0:T(8,128)(2,1)S(1)}, u32[]{:S(2)}) copy-start(bf16[22,224,128]{2,1,0:T(8,128)(2,1)S(1)} %collective-permute-done.1.east_p) | copy-start | bytes 3784708
  63.8 1.5 %copy-start = (bf16[24,224,128]{2,1,0:T(8,128)(2,1)}, bf16[24,224,128]{2,1,0:T(8,128)(2,1)S(1)}, u32[]{:S(2)}) copy-start(bf16[24,224,128]{2,1,0:T(8,128)(2,1)S(1)} %collective-permute-done.west_p) | copy-start | bytes 4128772
where the time goes:
time: 80.8 us; the launch traced here: 80.1 us
  starting transfers between devices  38.1 us (47%)
  waiting for transfers between devices  20.6 us (25%)
  Pallas kernels  18.4 us (23%)
  local copies, waits for them, and re-layouts  1.54 us (2%)
  other arithmetic  0.92 us (1%)
    ppermute x6, starting transfers between devices, passed_along(): return lax.ppermute(value, axis, pairs)  38.1 us
    ppermute x6, waiting for transfers between devices, passed_along(): return lax.ppermute(value, axis, pairs)  20.6 us
    pallas_call x1, Pallas kernels, chain(): pl.pallas_call(functools.partial(stencil_kernel, west_rows, east_rows), o...  14.9 us
    pallas_call x1, Pallas kernels, chain(): pl.pallas_call(functools.partial(pack_kernel, west_rows, east_rows), out_...  3.5 us
  transfers between devices with their start and end apart: 6, of which 3 were waited for; matrix products, arithmetic and copies ran while one was open for 1% of the time, Pallas kernels for 0%

commit v1 on v0

--- a/solution.py
+++ b/solution.py
@@ -6,6 +6,7 @@
 from jax.experimental import pallas as pl
 from jax.experimental.pallas import tpu as pltpu
 from jax.sharding import PartitionSpec as P
+
 
 HALO = 4
 PAD = 8
@@ -20,22 +21,41 @@
     return lax.ppermute(value, axis, pairs)
 
 
-def pack_kernel(west_rows, east_rows, conc, wind, kappa, observed, to_west, to_east, lows, highs):
-    fields = [conc, wind.at[0], wind.at[1], wind.at[2], kappa, observed]
-    size = conc.shape[0]
-    lats = conc.shape[1]
+def pack_kernel(west_rows, east_rows, conc, wind, kappa, observed, to_west, to_east, lows, highs,
+                split, edges, sems):
+    size, lats = conc.shape[0], conc.shape[1]
+    others = [wind.at[0], wind.at[1], wind.at[2], kappa, observed]
+    strip = edges.shape[2] // 2
+    copies = []
     for out, rows, first in ((to_west, east_rows, True), (to_east, west_rows, False)):
+        at = 2 * rows[0]
+        for f, r in zip(others, rows[1:]):
+            start = 0 if first else size - r
+            copies.append(pltpu.make_async_copy(f.at[pl.ds(start, r)], out.at[pl.ds(at, r)], sems.at[len(copies)]))
+            at += r
+    for n, f in enumerate(others):
+        for k, start in enumerate((0, lats - strip)):
+            dst = edges.at[n, :, pl.ds(k * strip, strip)]
+            copies.append(pltpu.make_async_copy(f.at[:, pl.ds(start, strip)], dst, sems.at[len(copies)]))
+    for c in copies:
+        c.start()
+    outs = []
+    for k, (out, rows, first) in enumerate(((to_west, east_rows, True), (to_east, west_rows, False))):
         part = conc[0:rows[0]] if first else conc[size - rows[0]:size]
         high = part.astype(jnp.bfloat16)
-        out[0:rows[0]] = high
-        out[rows[0]:2 * rows[0]] = (part - high.astype(jnp.float32)).astype(jnp.bfloat16)
-        at = 2 * rows[0]
-        for f, r in zip(fields[1:], rows[1:]):
-            out[at:at + r] = f[0:r] if first else f[size - r:size]
-            at += r
-    for n, f in enumerate(fields):
-        lows[n] = f[:, 0:HALO].astype(jnp.float32)
-        highs[n] = f[:, lats - HALO:lats].astype(jnp.float32)
+        split[k, 0:rows[0]] = high
+        split[k, rows[0]:2 * rows[0]] = (part - high.astype(jnp.float32)).astype(jnp.bfloat16)
+        outs.append(pltpu.make_async_copy(split.at[k], out.at[pl.ds(0, 2 * rows[0])], sems.at[len(copies) + k]))
+        outs[-1].start()
+    lows[0] = conc[:, 0:HALO]
+    highs[0] = conc[:, lats - HALO:lats]
+    for c in copies:
+        c.wait()
+    for n in range(len(others)):
+        lows[1 + n] = edges[n, :, 0:HALO].astype(jnp.float32)
+        highs[1 + n] = edges[n, :, 2 * strip - HALO:2 * strip].astype(jnp.float32)
+    for c in outs:
+        c.wait()
 
 
 def lat_halo(lows, highs, block):
@@ -198,8 +218,14 @@
             lat_type,
             lat_type,
         ),
-        in_specs=[pl.BlockSpec(memory_space=vmem)] * 4,
-        out_specs=tuple(pl.BlockSpec(memory_space=vmem) for _ in range(4)),
+        in_specs=[pl.BlockSpec(memory_space=vmem)] + [pl.BlockSpec(memory_space=pl.ANY)] * 3,
+        out_specs=(pl.BlockSpec(memory_space=pl.ANY), pl.BlockSpec(memory_space=pl.ANY),
+                   pl.BlockSpec(memory_space=vmem), pl.BlockSpec(memory_space=vmem)),
+        scratch_shapes=[
+            pltpu.VMEM((2, 2 * HALO, lat_rows, levels), jnp.bfloat16),
+            pltpu.VMEM((len(fields) - 1, lon_rows, 4 * HALO * 2, levels), jnp.bfloat16),
+            pltpu.SemaphoreType.DMA((32,)),
+        ],
     )(concentration, wind, kappa, observed)
     got = {"east": passed_along(to_west, "lon", -1, True), "west": passed_along(to_east, "lon", 1, True)}
     south, north = lat_halo(lows, highs, lon_rows)

time: 80.8 us -> 133 us (1.65)
  Pallas kernels: 18.4 us -> 70.3 us
    pallas_call x1, Pallas kernels: 3.5 us -> 55.4 us  [chain(): pl.pallas_call(functools.partial(pack_kernel, west_rows, east_rows), out_...]
where the time goes in v1:
time: 133 us; the launch traced here: 132 us
  Pallas kernels  70.3 us (53%)
  starting transfers between devices  38.1 us (29%)
  waiting for transfers between devices  20.6 us (15%)
  local copies, waits for them, and re-layouts  1.54 us (1%)
    pallas_call x1, Pallas kernels, chain(): pl.pallas_call(functools.partial(pack_kernel, west_rows, east_rows), out_...  55.4 us
    ppermute x6, starting transfers between devices, passed_along(): return lax.ppermute(value, axis, pairs)  38.1 us
    ppermute x6, waiting for transfers between devices, passed_along(): return lax.ppermute(value, axis, pairs)  20.6 us
    pallas_call x1, Pallas kernels, chain(): pl.pallas_call(functools.partial(stencil_kernel, west_rows, east_rows), o...  14.9 us
  transfers between devices with their start and end apart: 6, of which 3 were waited for; matrix products, arithmetic and copies ran while one was open for 1% of the time, Pallas kernels for 0%

profile of v1, /device:TPU:6, one launch (start us, length us, event | category | flops | bytes accessed | tf_op | source)
XLA Modules:
  0.0 132.1 jit_solution(17876174427268702792)
XLA Ops:
  0.6 55.4 %shard_map.59 = (bf16[22,224,128]{2,1,0:T(8,128)(2,1)}, bf16[24,224,128]{2,1,0:T(8,128)(2,1)}, f32[6,8,4,128]{3,2,1,0:T(4,128)}, f32[6,8,4,128]{3,2,1,0:T(4,128)}) custom-call(f32[8,224,128]{2,1,0:T(8,128)} %conc_in.1, bf16[3,8,224,128]{3,2,1,0:T(8,128)(2,1)} %wind_in.1, bf16[8,224,128]{2,1,0:T(8,128)(2,1)} %kappa_in.1, bf16[8,224,128]{2,1,0:T(8,128)(2,1)} %obs_in.1), custom_call_target="tpu_custom_call" | custom-call | tf_op jit(solution)/shard_map/pallas_call | solution.py:213
  56.0 1.9 %collective-permute-start = (bf16[24,224,128]{2,1,0:T(8,128)(2,1)}, bf16[24,224,128]{2,1,0:T(8,128)(2,1)S(1)}, u32[]{:S(2)}, u32[]{:S(2)}) collective-permute-start(bf16[24,224,128]{2,1,0:T(8,128)(2,1)} %get-tuple-element.6), channel_id=1, source_target_pairs={{0,8},{8,16},{16,24},{24,32},{32,40},{40,48},{48,56},{56,64},{64,7... | collective-permute-start | bytes 4128776 | tf_op jit(solution)/shard_map/ppermute | solution.py:21
  58.0 13.3 %collective-permute-start.1 = (bf16[22,224,128]{2,1,0:T(8,128)(2,1)}, bf16[22,224,128]{2,1,0:T(8,128)(2,1)S(1)}, u32[]{:S(2)}, u32[]{:S(2)}) collective-permute-start(bf16[22,224,128]{2,1,0:T(8,128)(2,1)} %get-tuple-element.7), channel_id=1, source_target_pairs={{0,504},{8,0},{16,8},{24,16},{32,24},{40,32},{48,40},{56,48},{64,5... | collective-permute-start | bytes 3784712 | tf_op jit(solution)/shard_map/ppermute | solution.py:21
  71.3 3.3 %collective-permute-start.2 = (f32[6,8,4,128]{3,2,1,0:T(4,128)}, f32[6,8,4,128]{3,2,1,0:T(4,128)S(1)}, u32[]{:S(2)}, u32[]{:S(2)}) collective-permute-start(f32[6,8,4,128]{3,2,1,0:T(4,128)} %get-tuple-element.8), channel_id=1, source_target_pairs={{0,1},{1,2},{2,3},{3,4},{4,5},{5,6},{6,7},{8,9},{9,10},{10,11},{11... | collective-permute-start | bytes 294920 | tf_op jit(solution)/shard_map/ppermute | solution.py:21
  74.6 2.5 %collective-permute-start.3 = (f32[6,8,4,128]{3,2,1,0:T(4,128)}, f32[6,8,4,128]{3,2,1,0:T(4,128)S(1)}, u32[]{:S(2)}, u32[]{:S(2)}) collective-permute-start(f32[6,8,4,128]{3,2,1,0:T(4,128)} %get-tuple-element.9), channel_id=1, source_target_pairs={{1,0},{2,1},{3,2},{4,3},{5,4},{6,5},{7,6},{9,8},{10,9},{11,10},{12... | collective-permute-start | bytes 294920 | tf_op jit(solution)/shard_map/ppermute | solution.py:21
  77.1 18.4 %collective-permute-done.2 = f32[6,8,4,128]{3,2,1,0:T(4,128)S(1)} collective-permute-done((f32[6,8,4,128]{3,2,1,0:T(4,128)}, f32[6,8,4,128]{3,2,1,0:T(4,128)S(1)}, u32[]{:S(2)}, u32[]{:S(2)}) %collective-permute-start.2) | collective-permute-done | bytes 98336 | tf_op jit(solution)/shard_map/ppermute | solution.py:21
  95.5 0.0 collective-permute-done.3
  95.5 1.9 %collective-permute-start.4 = (f32[2,6,4,4,128]{4,3,2,1,0:T(4,128)S(1)}, f32[2,6,4,4,128]{4,3,2,1,0:T(4,128)S(1)}, u32[]{:S(2)}, u32[]{:S(2)}) collective-permute-start(f32[2,6,4,4,128]{4,3,2,1,0:T(4,128)S(1)} %get-tuple-element.10), channel_id=1, source_target_pairs={{0,8},{8,16},{16,24},{24,32},{32,40},{40,48},{48,56},{56,64},{64,7... | collective-permute-start | bytes 294920 | tf_op jit(solution)/shard_map/ppermute | solution.py:21
  97.5 15.1 %collective-permute-start.5 = (f32[2,6,4,4,128]{4,3,2,1,0:T(4,128)S(1)}, f32[2,6,4,4,128]{4,3,2,1,0:T(4,128)S(1)}, u32[]{:S(2)}, u32[]{:S(2)}) collective-permute-start(f32[2,6,4,4,128]{4,3,2,1,0:T(4,128)S(1)} %get-tuple-element.11), channel_id=1, source_target_pairs={{0,504},{8,0},{16,8},{24,16},{32,24},{40,32},{48,40},{56,48},{64,5... | collective-permute-start | bytes 294920 | tf_op jit(solution)/shard_map/ppermute | solution.py:21
  112.6 0.3 collective-permute-done.4
  113.0 1.8 %collective-permute-done.5 = f32[2,6,4,4,128]{4,3,2,1,0:T(4,128)S(1)} collective-permute-done((f32[2,6,4,4,128]{4,3,2,1,0:T(4,128)S(1)}, f32[2,6,4,4,128]{4,3,2,1,0:T(4,128)S(1)}, u32[]{:S(2)}, u32[]{:S(2)}) %collective-permute-start.5) | collective-permute-done | bytes 98336 | tf_op jit(solution)/shard_map/ppermute | solution.py:21
  114.8 0.9 pad_maximum_fusion
  115.7 0.0 collective-permute-done.1.east_p
  115.7 0.0 copy-start.1
  115.7 0.0 collective-permute-done.west_p
  115.7 0.0 copy-start
  115.7 0.9 iota.7.north_ref
  116.5 0.2 copy-done.1
  116.7 0.5 copy-done
  117.2 14.9 %shard_map.60 = (f32[8,224,128]{2,1,0:T(8,128)}, f32[8,224,128]{2,1,0:T(8,128)}) custom-call(f32[8,224,128]{2,1,0:T(8,128)} %conc_in.1, bf16[3,8,224,128]{3,2,1,0:T(8,128)(2,1)} %wind_in.1, bf16[8,224,128]{2,1,0:T(8,128)(2,1)} %kappa_in.1, bf16[8,224,128]{2,1,0:T(8,128)(2,1)} %obs_in.1, bf16[24,224,128]{2,1,0:T(8,128)(2,1)} %copy-done, ...), custom_call_target="tpu_custom_call" | custom-call | tf_op jit(solution)/shard_map/pallas_call | solution.py:239
  (4 shorter events, 0.1 us)
Async XLA Ops:
  56.0 59.6 %collective-permute-start = (bf16[24,224,128]{2,1,0:T(8,128)(2,1)}, bf16[24,224,128]{2,1,0:T(8,128)(2,1)S(1)}, u32[]{:S(2)}, u32[]{:S(2)}) collective-permute-start(bf16[24,224,128]{2,1,0:T(8,128)(2,1)} %get-tuple-element.6), channel_id=1, source_target_pairs={{0,8},{8,16},{16,24},{24,32},{32,40},{40,48},{48,56},{56,64},{64,7... | collective-permute-start | bytes 4128776 | tf_op jit(solution)/shard_map/ppermute | solution.py:21
  58.0 57.7 %collective-permute-start.1 = (bf16[22,224,128]{2,1,0:T(8,128)(2,1)}, bf16[22,224,128]{2,1,0:T(8,128)(2,1)S(1)}, u32[]{:S(2)}, u32[]{:S(2)}) collective-permute-start(bf16[22,224,128]{2,1,0:T(8,128)(2,1)} %get-tuple-element.7), channel_id=1, source_target_pairs={{0,504},{8,0},{16,8},{24,16},{32,24},{40,32},{48,40},{56,48},{64,5... | collective-permute-start | bytes 3784712 | tf_op jit(solution)/shard_map/ppermute | solution.py:21
  71.3 24.2 %collective-permute-start.2 = (f32[6,8,4,128]{3,2,1,0:T(4,128)}, f32[6,8,4,128]{3,2,1,0:T(4,128)S(1)}, u32[]{:S(2)}, u32[]{:S(2)}) collective-permute-start(f32[6,8,4,128]{3,2,1,0:T(4,128)} %get-tuple-element.8), channel_id=1, source_target_pairs={{0,1},{1,2},{2,3},{3,4},{4,5},{5,6},{6,7},{8,9},{9,10},{10,11},{11... | collective-permute-start | bytes 294920 | tf_op jit(solution)/shard_map/ppermute | solution.py:21
  74.6 20.9 %collective-permute-start.3 = (f32[6,8,4,128]{3,2,1,0:T(4,128)}, f32[6,8,4,128]{3,2,1,0:T(4,128)S(1)}, u32[]{:S(2)}, u32[]{:S(2)}) collective-permute-start(f32[6,8,4,128]{3,2,1,0:T(4,128)} %get-tuple-element.9), channel_id=1, source_target_pairs={{1,0},{2,1},{3,2},{4,3},{5,4},{6,5},{7,6},{9,8},{10,9},{11,10},{12... | collective-permute-start | bytes 294920 | tf_op jit(solution)/shard_map/ppermute | solution.py:21
  95.5 17.4 %collective-permute-start.4 = (f32[2,6,4,4,128]{4,3,2,1,0:T(4,128)S(1)}, f32[2,6,4,4,128]{4,3,2,1,0:T(4,128)S(1)}, u32[]{:S(2)}, u32[]{:S(2)}) collective-permute-start(f32[2,6,4,4,128]{4,3,2,1,0:T(4,128)S(1)} %get-tuple-element.10), channel_id=1, source_target_pairs={{0,8},{8,16},{16,24},{24,32},{32,40},{40,48},{48,56},{56,64},{64,7... | collective-permute-start | bytes 294920 | tf_op jit(solution)/shard_map/ppermute | solution.py:21
  97.5 17.3 %collective-permute-start.5 = (f32[2,6,4,4,128]{4,3,2,1,0:T(4,128)S(1)}, f32[2,6,4,4,128]{4,3,2,1,0:T(4,128)S(1)}, u32[]{:S(2)}, u32[]{:S(2)}) collective-permute-start(f32[2,6,4,4,128]{4,3,2,1,0:T(4,128)S(1)} %get-tuple-element.11), channel_id=1, source_target_pairs={{0,504},{8,0},{16,8},{24,16},{32,24},{40,32},{48,40},{56,48},{64,5... | collective-permute-start | bytes 294920 | tf_op jit(solution)/shard_map/ppermute | solution.py:21
  115.7 1.1 copy-start.1
  115.7 1.5 %copy-start = (bf16[24,224,128]{2,1,0:T(8,128)(2,1)}, bf16[24,224,128]{2,1,0:T(8,128)(2,1)S(1)}, u32[]{:S(2)}) copy-start(bf16[24,224,128]{2,1,0:T(8,128)(2,1)S(1)} %collective-permute-done.west_p) | copy-start | bytes 4128772

commit v2 on v0

--- a/solution.py
+++ b/solution.py
@@ -6,6 +6,7 @@
 from jax.experimental import pallas as pl
 from jax.experimental.pallas import tpu as pltpu
 from jax.sharding import PartitionSpec as P
+
 
 HALO = 4
 PAD = 8
@@ -44,48 +45,49 @@
     both = jnp.stack([from_south, from_north])
     west = passed_along(both[:, :, block - HALO:], "lon", 1, True)
     east = passed_along(both[:, :, :HALO], "lon", -1, True)
-    return [jnp.concatenate([west[n], both[n], east[n]], 1) for n in range(2)]
-
-
-def stencil_kernel(west_rows, east_rows, conc_in, wind_in, kappa_in, obs_in, west_p, east_p,
-                   south_ref, north_halo, north_ref, gc_ref, gk_ref, raw_ref, own_ref, oth_ref, mid_ref, lam2_ref,
-                   lam1_ref):
+    return west, both, east
+
+
+def stencil_kernel(west_rows, east_rows, lat_limits, conc_in, wind_in, kappa_in, obs_in, west_p, east_p,
+                   corner_w, lat_own, corner_e, place_ref, gc_ref, gk_ref, raw_ref, own_ref, oth_ref, mid_ref,
+                   lam2_ref, lam1_ref):
     fields, rows, lats, levels = raw_ref.shape
     block = conc_in.shape[0]
     f32 = jnp.float32
-    north_open = north_ref[...]
+    lat_place = place_ref[0] + lax.broadcasted_iota(jnp.int32, (lats, levels), 0)
+    north_open = ((lat_place >= 0) & (lat_place < lat_limits - 1)).astype(f32)
     lo = PAD
     hi = lats - PAD
     gap = jnp.zeros((PAD - HALO, levels), f32)
 
-    def put(f, r, core):
+    def put(f, r, core, halo, at):
         raw_ref[f, r, lo:hi] = core
-        raw_ref[f, r, lo - HALO:lo] = south_ref[f, r]
-        raw_ref[f, r, hi:hi + HALO] = north_halo[f, r]
+        raw_ref[f, r, lo - HALO:lo] = halo[0, f, at]
+        raw_ref[f, r, hi:hi + HALO] = halo[1, f, at]
         raw_ref[f, r, :lo - HALO] = gap
         raw_ref[f, r, hi + HALO:] = gap
 
     def own_row(i, carry):
-        put(0, i + HALO, conc_in[i])
+        put(0, i + HALO, conc_in[i], lat_own, i)
         for d in range(3):
-            put(1 + d, i + HALO, wind_in[d, i].astype(f32))
-        put(4, i + HALO, kappa_in[i].astype(f32))
-        put(5, i + HALO, obs_in[i].astype(f32))
+            put(1 + d, i + HALO, wind_in[d, i].astype(f32), lat_own, i)
+        put(4, i + HALO, kappa_in[i].astype(f32), lat_own, i)
+        put(5, i + HALO, obs_in[i].astype(f32), lat_own, i)
         return carry
 
     lax.fori_loop(0, block, own_row, 0)
     empty = jnp.zeros((hi - lo, levels), f32)
     for r in range(HALO):
-        put(0, r, west_p[r].astype(f32) + west_p[HALO + r].astype(f32))
-        put(0, HALO + block + r, east_p[r].astype(f32) + east_p[HALO + r].astype(f32))
+        put(0, r, west_p[r].astype(f32) + west_p[HALO + r].astype(f32), corner_w, r)
+        put(0, HALO + block + r, east_p[r].astype(f32) + east_p[HALO + r].astype(f32), corner_e, r)
     at_w = 2 * HALO
     at_e = 2 * HALO
     for f in range(1, fields):
         w = west_rows[f]
         e = east_rows[f]
         for r in range(HALO):
-            put(f, r, west_p[at_w + r - (HALO - w)].astype(f32) if r >= HALO - w else empty)
-            put(f, HALO + block + r, east_p[at_e + r].astype(f32) if r < e else empty)
+            put(f, r, west_p[at_w + r - (HALO - w)].astype(f32) if r >= HALO - w else empty, corner_w, r)
+            put(f, HALO + block + r, east_p[at_e + r].astype(f32) if r < e else empty, corner_e, r)
         at_w += w
         at_e += e
     conc_ref = raw_ref.at[0]
@@ -202,21 +204,20 @@
         out_specs=tuple(pl.BlockSpec(memory_space=vmem) for _ in range(4)),
     )(concentration, wind, kappa, observed)
     got = {"east": passed_along(to_west, "lon", -1, True), "west": passed_along(to_east, "lon", 1, True)}
-    south, north = lat_halo(lows, highs, lon_rows)
+    corner_w, lat_own, corner_e = lat_halo(lows, highs, lon_rows)
     ext_rows = lon_rows + 2 * HALO
     ext_lats = lat_rows + 2 * PAD
-    lat_place = lax.axis_index("lat") * lat_rows - PAD + lax.broadcasted_iota(jnp.int32, (ext_lats, levels), 0)
-    north_open = ((lat_place >= 0) & (lat_place < lat_total - 1)).astype(jnp.float32)
-    whole = [concentration, wind, kappa, observed, got["west"], got["east"], south, north, north_open]
+    place = jnp.reshape(lax.axis_index("lat") * lat_rows - PAD, (1,)).astype(jnp.int32)
+    whole = [concentration, wind, kappa, observed, got["west"], got["east"], corner_w, lat_own, corner_e]
     vmem = pltpu.MemorySpace.VMEM
     state = pltpu.VMEM((ext_rows, ext_lats, levels), jnp.float32)
     return pl.pallas_call(
-        functools.partial(stencil_kernel, west_rows, east_rows),
+        functools.partial(stencil_kernel, west_rows, east_rows, lat_total),
         out_shape=(
             jax.ShapeDtypeStruct((lon_rows, lat_rows, levels), jnp.float32),
             jax.ShapeDtypeStruct((lon_rows, lat_rows, levels), jnp.float32),
         ),
-        in_specs=[pl.BlockSpec(memory_space=vmem) for _ in whole],
+        in_specs=[pl.BlockSpec(memory_space=vmem) for _ in whole] + [pl.BlockSpec(memory_space=pltpu.SMEM)],
         out_specs=(pl.BlockSpec(memory_space=vmem), pl.BlockSpec(memory_space=vmem)),
         scratch_shapes=[
             pltpu.VMEM((len(fields), ext_rows, ext_lats, levels), jnp.float32),
@@ -227,7 +228,7 @@
             state,
         ],
         compiler_params=pltpu.CompilerParams(vmem_limit_bytes=60 * 1024 * 1024),
-    )(*whole)
+    )(*whole, place)
 
 
 def solution(mesh):

time: 80.8 us -> 85.5 us (1.058)
  waiting for transfers between devices: 20.6 us -> 25.9 us
    ppermute x6, waiting for transfers between devices: 20.6 us -> 25.9 us  [passed_along(): return lax.ppermute(value, axis, pairs)]
    concatenate x1 -> x0, other arithmetic: 0.86 us -> none  [lat_halo(): return [jnp.concatenate([west[n], both[n], east[n]], 1) for n in range(2)]]
    iota x1 -> x0, local copies, waits for them, and re-layouts: 0.86 us -> none  [chain(): lax.broadcasted_iota(jnp.int32, (ext_lats, levels), 0)]
  transfers between devices with their start and end apart: 6 -> 6, of which waited for: 3 -> 2; matrix products, arithmetic and copies ran while one was open for 1% -> 1% of each run, Pallas kernels for 0% -> 0%
where the time goes in v2:
time: 85.5 us; the launch traced here: 85.3 us
  starting transfers between devices  38.1 us (45%)
  waiting for transfers between devices  25.9 us (30%)
  Pallas kernels  18.4 us (22%)
  local copies, waits for them, and re-layouts  1.49 us (2%)
    ppermute x6, starting transfers between devices, passed_along(): return lax.ppermute(value, axis, pairs)  38.1 us
    ppermute x6, waiting for transfers between devices, passed_along(): return lax.ppermute(value, axis, pairs)  25.9 us
    pallas_call x1, Pallas kernels, chain(): pl.pallas_call(functools.partial(stencil_kernel, west_rows, east_rows, la...  14.9 us
    pallas_call x1, Pallas kernels, chain(): pl.pallas_call(functools.partial(pack_kernel, west_rows, east_rows), out_...  3.5 us
  transfers between devices with their start and end apart: 6, of which 2 were waited for; matrix products, arithmetic and copies ran while one was open for 1% of the time, Pallas kernels for 0%

profile of v2, /device:TPU:6, one launch (start us, length us, event | category | flops | bytes accessed | tf_op | source)
XLA Modules:
  0.0 85.3 jit_solution(5865848417209749090)
XLA Ops:
  0.6 3.5 %shard_map.59 = (bf16[22,224,128]{2,1,0:T(8,128)(2,1)}, bf16[24,224,128]{2,1,0:T(8,128)(2,1)}, f32[6,8,4,128]{3,2,1,0:T(4,128)}, f32[6,8,4,128]{3,2,1,0:T(4,128)}) custom-call(f32[8,224,128]{2,1,0:T(8,128)} %conc_in.1, bf16[3,8,224,128]{3,2,1,0:T(8,128)(2,1)} %wind_in.1, bf16[8,224,128]{2,1,0:T(8,128)(2,1)} %kappa_in.1, bf16[8,224,128]{2,1,0:T(8,128)(2,1)} %obs_in.1), custom_call_target="tpu_custom_call" | custom-call | tf_op jit(solution)/shard_map/pallas_call | solution.py:195
  4.1 1.9 %collective-permute-start = (bf16[24,224,128]{2,1,0:T(8,128)(2,1)}, bf16[24,224,128]{2,1,0:T(8,128)(2,1)S(1)}, u32[]{:S(2)}, u32[]{:S(2)}) collective-permute-start(bf16[24,224,128]{2,1,0:T(8,128)(2,1)} %get-tuple-element.6), channel_id=1, source_target_pairs={{0,8},{8,16},{16,24},{24,32},{32,40},{40,48},{48,56},{56,64},{64,7... | collective-permute-start | bytes 4128776 | tf_op jit(solution)/shard_map/ppermute | solution.py:21
  6.0 13.3 %collective-permute-start.1 = (bf16[22,224,128]{2,1,0:T(8,128)(2,1)}, bf16[22,224,128]{2,1,0:T(8,128)(2,1)S(1)}, u32[]{:S(2)}, u32[]{:S(2)}) collective-permute-start(bf16[22,224,128]{2,1,0:T(8,128)(2,1)} %get-tuple-element.7), channel_id=1, source_target_pairs={{0,504},{8,0},{16,8},{24,16},{32,24},{40,32},{48,40},{56,48},{64,5... | collective-permute-start | bytes 3784712 | tf_op jit(solution)/shard_map/ppermute | solution.py:21
  19.3 3.3 %collective-permute-start.2 = (f32[6,8,4,128]{3,2,1,0:T(4,128)}, f32[6,8,4,128]{3,2,1,0:T(4,128)S(1)}, u32[]{:S(2)}, u32[]{:S(2)}) collective-permute-start(f32[6,8,4,128]{3,2,1,0:T(4,128)} %get-tuple-element.8), channel_id=1, source_target_pairs={{0,1},{1,2},{2,3},{3,4},{4,5},{5,6},{6,7},{8,9},{9,10},{10,11},{11... | collective-permute-start | bytes 294920 | tf_op jit(solution)/shard_map/ppermute | solution.py:21
  22.6 2.5 %collective-permute-start.3 = (f32[6,8,4,128]{3,2,1,0:T(4,128)}, f32[6,8,4,128]{3,2,1,0:T(4,128)S(1)}, u32[]{:S(2)}, u32[]{:S(2)}) collective-permute-start(f32[6,8,4,128]{3,2,1,0:T(4,128)} %get-tuple-element.9), channel_id=1, source_target_pairs={{1,0},{2,1},{3,2},{4,3},{5,4},{6,5},{7,6},{9,8},{10,9},{11,10},{12... | collective-permute-start | bytes 294920 | tf_op jit(solution)/shard_map/ppermute | solution.py:21
  25.2 18.4 %collective-permute-done.2 = f32[6,8,4,128]{3,2,1,0:T(4,128)S(1)} collective-permute-done((f32[6,8,4,128]{3,2,1,0:T(4,128)}, f32[6,8,4,128]{3,2,1,0:T(4,128)S(1)}, u32[]{:S(2)}, u32[]{:S(2)}) %collective-permute-start.2) | collective-permute-done | bytes 98336 | tf_op jit(solution)/shard_map/ppermute | solution.py:21
  43.6 0.0 collective-permute-done.3
  43.6 15.1 %collective-permute-start.5 = (f32[2,6,4,4,128]{4,3,2,1,0:T(4,128)S(1)}, f32[2,6,4,4,128]{4,3,2,1,0:T(4,128)S(1)}, u32[]{:S(2)}, u32[]{:S(2)}) collective-permute-start(f32[2,6,4,4,128]{4,3,2,1,0:T(4,128)S(1)} %get-tuple-element.10), channel_id=1, source_target_pairs={{0,504},{8,0},{16,8},{24,16},{32,24},{40,32},{48,40},{56,48},{64,5... | collective-permute-start | bytes 294920 | tf_op jit(solution)/shard_map/ppermute | solution.py:21
  58.7 1.9 %collective-permute-start.4 = (f32[2,6,4,4,128]{4,3,2,1,0:T(4,128)S(1)}, f32[2,6,4,4,128]{4,3,2,1,0:T(4,128)S(1)}, u32[]{:S(2)}, u32[]{:S(2)}) collective-permute-start(f32[2,6,4,4,128]{4,3,2,1,0:T(4,128)S(1)} %get-tuple-element.11), channel_id=1, source_target_pairs={{0,8},{8,16},{16,24},{24,32},{32,40},{40,48},{48,56},{56,64},{64,7... | collective-permute-start | bytes 294920 | tf_op jit(solution)/shard_map/ppermute | solution.py:21
  60.7 0.7 pad_maximum_fusion.lat_own
  61.4 0.0 collective-permute-done.5.corner_e
  61.4 0.0 copy-start.2
  61.4 7.5 %collective-permute-done.4.corner_w = f32[2,6,4,4,128]{4,3,2,1,0:T(4,128)S(1)} collective-permute-done((f32[2,6,4,4,128]{4,3,2,1,0:T(4,128)S(1)}, f32[2,6,4,4,128]{4,3,2,1,0:T(4,128)S(1)}, u32[]{:S(2)}, u32[]{:S(2)}) %collective-permute-start.4) | collective-permute-done | bytes 98336 | tf_op jit(solution)/shard_map/ppermute | solution.py:21
  68.9 0.0 copy-start.3
  68.9 0.0 collective-permute-done.1.east_p
  68.9 0.0 copy-start.1
  68.9 0.0 collective-permute-done.west_p
  68.9 0.0 copy-start
  68.9 0.0 copy-done.2
  68.9 0.6 copy-done.3
  69.5 0.4 copy-done.1
  70.0 0.4 copy-done
  70.4 14.9 %shard_map.60 = (f32[8,224,128]{2,1,0:T(8,128)}, f32[8,224,128]{2,1,0:T(8,128)}) custom-call(f32[8,224,128]{2,1,0:T(8,128)} %conc_in.1, bf16[3,8,224,128]{3,2,1,0:T(8,128)(2,1)} %wind_in.1, bf16[8,224,128]{2,1,0:T(8,128)(2,1)} %kappa_in.1, bf16[8,224,128]{2,1,0:T(8,128)(2,1)} %obs_in.1, bf16[24,224,128]{2,1,0:T(8,128)(2,1)} %copy-done, ...), custom_call_target="tpu_custom_call" | custom-call | tf_op jit(solution)/shard_map/pallas_call | solution.py:214
  (1 shorter events, 0.0 us)
Async XLA Ops:
  4.1 64.8 %collective-permute-start = (bf16[24,224,128]{2,1,0:T(8,128)(2,1)}, bf16[24,224,128]{2,1,0:T(8,128)(2,1)S(1)}, u32[]{:S(2)}, u32[]{:S(2)}) collective-permute-start(bf16[24,224,128]{2,1,0:T(8,128)(2,1)} %get-tuple-element.6), channel_id=1, source_target_pairs={{0,8},{8,16},{16,24},{24,32},{32,40},{40,48},{48,56},{56,64},{64,7... | collective-permute-start | bytes 4128776 | tf_op jit(solution)/shard_map/ppermute | solution.py:21
  6.0 62.9 %collective-permute-start.1 = (bf16[22,224,128]{2,1,0:T(8,128)(2,1)}, bf16[22,224,128]{2,1,0:T(8,128)(2,1)S(1)}, u32[]{:S(2)}, u32[]{:S(2)}) collective-permute-start(bf16[22,224,128]{2,1,0:T(8,128)(2,1)} %get-tuple-element.7), channel_id=1, source_target_pairs={{0,504},{8,0},{16,8},{24,16},{32,24},{40,32},{48,40},{56,48},{64,5... | collective-permute-start | bytes 3784712 | tf_op jit(solution)/shard_map/ppermute | solution.py:21
  19.3 24.2 %collective-permute-start.2 = (f32[6,8,4,128]{3,2,1,0:T(4,128)}, f32[6,8,4,128]{3,2,1,0:T(4,128)S(1)}, u32[]{:S(2)}, u32[]{:S(2)}) collective-permute-start(f32[6,8,4,128]{3,2,1,0:T(4,128)} %get-tuple-element.8), channel_id=1, source_target_pairs={{0,1},{1,2},{2,3},{3,4},{4,5},{5,6},{6,7},{8,9},{9,10},{10,11},{11... | collective-permute-start | bytes 294920 | tf_op jit(solution)/shard_map/ppermute | solution.py:21
  22.6 20.9 %collective-permute-start.3 = (f32[6,8,4,128]{3,2,1,0:T(4,128)}, f32[6,8,4,128]{3,2,1,0:T(4,128)S(1)}, u32[]{:S(2)}, u32[]{:S(2)}) collective-permute-start(f32[6,8,4,128]{3,2,1,0:T(4,128)} %get-tuple-element.9), channel_id=1, source_target_pairs={{1,0},{2,1},{3,2},{4,3},{5,4},{6,5},{7,6},{9,8},{10,9},{11,10},{12... | collective-permute-start | bytes 294920 | tf_op jit(solution)/shard_map/ppermute | solution.py:21
  43.6 17.8 %collective-permute-start.5 = (f32[2,6,4,4,128]{4,3,2,1,0:T(4,128)S(1)}, f32[2,6,4,4,128]{4,3,2,1,0:T(4,128)S(1)}, u32[]{:S(2)}, u32[]{:S(2)}) collective-permute-start(f32[2,6,4,4,128]{4,3,2,1,0:T(4,128)S(1)} %get-tuple-element.10), channel_id=1, source_target_pairs={{0,504},{8,0},{16,8},{24,16},{32,24},{40,32},{48,40},{56,48},{64,5... | collective-permute-start | bytes 294920 | tf_op jit(solution)/shard_map/ppermute | solution.py:21
  58.7 10.2 %collective-permute-start.4 = (f32[2,6,4,4,128]{4,3,2,1,0:T(4,128)S(1)}, f32[2,6,4,4,128]{4,3,2,1,0:T(4,128)S(1)}, u32[]{:S(2)}, u32[]{:S(2)}) collective-permute-start(f32[2,6,4,4,128]{4,3,2,1,0:T(4,128)S(1)} %get-tuple-element.11), channel_id=1, source_target_pairs={{0,8},{8,16},{16,24},{24,32},{32,40},{40,48},{48,56},{56,64},{64,7... | collective-permute-start | bytes 294920 | tf_op jit(solution)/shard_map/ppermute | solution.py:21
  61.4 7.5 %copy-start.2 = (f32[2,6,4,4,128]{4,3,2,1,0:T(4,128)}, f32[2,6,4,4,128]{4,3,2,1,0:T(4,128)S(1)}, u32[]{:S(2)}) copy-start(f32[2,6,4,4,128]{4,3,2,1,0:T(4,128)S(1)} %collective-permute-done.5.corner_e) | copy-start | bytes 294916
  68.9 0.6 copy-start.3
  68.9 1.1 %copy-start.1 = (bf16[22,224,128]{2,1,0:T(8,128)(2,1)}, bf16[22,224,128]{2,1,0:T(8,128)(2,1)S(1)}, u32[]{:S(2)}) copy-start(bf16[22,224,128]{2,1,0:T(8,128)(2,1)S(1)} %collective-permute-done.1.east_p) | copy-start | bytes 3784708
  68.9 1.5 %copy-start = (bf16[24,224,128]{2,1,0:T(8,128)(2,1)}, bf16[24,224,128]{2,1,0:T(8,128)(2,1)S(1)}, u32[]{:S(2)}) copy-start(bf16[24,224,128]{2,1,0:T(8,128)(2,1)S(1)} %collective-permute-done.west_p) | copy-start | bytes 4128772

commit v3 on v2

--- a/solution.py
+++ b/solution.py
@@ -29,8 +29,9 @@
         part = conc[0:rows[0]] if first else conc[size - rows[0]:size]
         high = part.astype(jnp.bfloat16)
         out[0:rows[0]] = high
-        out[rows[0]:2 * rows[0]] = (part - high.astype(jnp.float32)).astype(jnp.bfloat16)
-        at = 2 * rows[0]
+        low = (part - high.astype(jnp.float32)).astype(jnp.bfloat16)
+        out[rows[0]:2 * rows[0] - 1] = low[0:rows[0] - 1] if first else low[1:rows[0]]
+        at = 2 * rows[0] - 1
         for f, r in zip(fields[1:], rows[1:]):
             out[at:at + r] = f[0:r] if first else f[size - r:size]
             at += r
@@ -78,10 +79,16 @@
     lax.fori_loop(0, block, own_row, 0)
     empty = jnp.zeros((hi - lo, levels), f32)
     for r in range(HALO):
-        put(0, r, west_p[r].astype(f32) + west_p[HALO + r].astype(f32), corner_w, r)
-        put(0, HALO + block + r, east_p[r].astype(f32) + east_p[HALO + r].astype(f32), corner_e, r)
-    at_w = 2 * HALO
-    at_e = 2 * HALO
+        west_c = west_p[r].astype(f32)
+        if r >= 1:
+            west_c = west_c + west_p[HALO + r - 1].astype(f32)
+        east_c = east_p[r].astype(f32)
+        if r < HALO - 1:
+            east_c = east_c + east_p[HALO + r].astype(f32)
+        put(0, r, west_c, corner_w, r)
+        put(0, HALO + block + r, east_c, corner_e, r)
+    at_w = 2 * HALO - 1
+    at_e = 2 * HALO - 1
     for f in range(1, fields):
         w = west_rows[f]
         e = east_rows[f]
@@ -190,7 +197,7 @@
     west_rows = (4, 4, 3, 3, 4, 2)
     east_rows = (4, 3, 3, 3, 3, 2)
     vmem = pltpu.MemorySpace.VMEM
-    pack_rows = lambda rows: 2 * rows[0] + sum(rows[1:])
+    pack_rows = lambda rows: 2 * rows[0] - 1 + sum(rows[1:])
     lat_type = jax.ShapeDtypeStruct((len(fields), lon_rows, HALO, levels), jnp.float32)
     to_west, to_east, lows, highs = pl.pallas_call(
         functools.partial(pack_kernel, west_rows, east_rows),

time: 85.5 us -> 84.2 us (0.985)
  waiting for transfers between devices: 25.9 us -> 24.6 us
    ppermute x6, waiting for transfers between devices: 25.9 us -> 24.6 us  [passed_along(): return lax.ppermute(value, axis, pairs)]
where the time goes in v3:
time: 84.2 us; the launch traced here: 83.9 us
  starting transfers between devices  38.1 us (45%)
  waiting for transfers between devices  24.6 us (29%)
  Pallas kernels  18.3 us (22%)
  local copies, waits for them, and re-layouts  1.47 us (2%)
    ppermute x6, starting transfers between devices, passed_along(): return lax.ppermute(value, axis, pairs)  38.1 us
    ppermute x6, waiting for transfers between devices, passed_along(): return lax.ppermute(value, axis, pairs)  24.6 us
    pallas_call x1, Pallas kernels, chain(): pl.pallas_call(functools.partial(stencil_kernel, west_rows, east_rows, la...  14.8 us
    pallas_call x1, Pallas kernels, chain(): pl.pallas_call(functools.partial(pack_kernel, west_rows, east_rows), out_...  3.46 us
  transfers between devices with their start and end apart: 6, of which 2 were waited for; matrix products, arithmetic and copies ran while one was open for 1% of the time, Pallas kernels for 0%

profile of v3, /device:TPU:6, one launch (start us, length us, event | category | flops | bytes accessed | tf_op | source)
XLA Modules:
  0.0 83.9 jit_solution(6114968843643348754)
XLA Ops:
  0.6 3.5 %shard_map.59 = (bf16[21,224,128]{2,1,0:T(8,128)(2,1)}, bf16[23,224,128]{2,1,0:T(8,128)(2,1)}, f32[6,8,4,128]{3,2,1,0:T(4,128)}, f32[6,8,4,128]{3,2,1,0:T(4,128)}) custom-call(f32[8,224,128]{2,1,0:T(8,128)} %conc_in.1, bf16[3,8,224,128]{3,2,1,0:T(8,128)(2,1)} %wind_in.1, bf16[8,224,128]{2,1,0:T(8,128)(2,1)} %kappa_in.1, bf16[8,224,128]{2,1,0:T(8,128)(2,1)} %obs_in.1), custom_call_target="tpu_custom_call" | custom-call | tf_op jit(solution)/shard_map/pallas_call | solution.py:202
  4.1 1.9 %collective-permute-start = (bf16[23,224,128]{2,1,0:T(8,128)(2,1)}, bf16[23,224,128]{2,1,0:T(8,128)(2,1)S(1)}, u32[]{:S(2)}, u32[]{:S(2)}) collective-permute-start(bf16[23,224,128]{2,1,0:T(8,128)(2,1)} %get-tuple-element.6), channel_id=1, source_target_pairs={{0,8},{8,16},{16,24},{24,32},{32,40},{40,48},{48,56},{56,64},{64,7... | collective-permute-start | bytes 3956744 | tf_op jit(solution)/shard_map/ppermute | solution.py:21
  6.0 13.3 %collective-permute-start.1 = (bf16[21,224,128]{2,1,0:T(8,128)(2,1)}, bf16[21,224,128]{2,1,0:T(8,128)(2,1)S(1)}, u32[]{:S(2)}, u32[]{:S(2)}) collective-permute-start(bf16[21,224,128]{2,1,0:T(8,128)(2,1)} %get-tuple-element.7), channel_id=1, source_target_pairs={{0,504},{8,0},{16,8},{24,16},{32,24},{40,32},{48,40},{56,48},{64,5... | collective-permute-start | bytes 3612680 | tf_op jit(solution)/shard_map/ppermute | solution.py:21
  19.3 3.3 %collective-permute-start.2 = (f32[6,8,4,128]{3,2,1,0:T(4,128)}, f32[6,8,4,128]{3,2,1,0:T(4,128)S(1)}, u32[]{:S(2)}, u32[]{:S(2)}) collective-permute-start(f32[6,8,4,128]{3,2,1,0:T(4,128)} %get-tuple-element.8), channel_id=1, source_target_pairs={{0,1},{1,2},{2,3},{3,4},{4,5},{5,6},{6,7},{8,9},{9,10},{10,11},{11... | collective-permute-start | bytes 294920 | tf_op jit(solution)/shard_map/ppermute | solution.py:21
  22.6 2.5 %collective-permute-start.3 = (f32[6,8,4,128]{3,2,1,0:T(4,128)}, f32[6,8,4,128]{3,2,1,0:T(4,128)S(1)}, u32[]{:S(2)}, u32[]{:S(2)}) collective-permute-start(f32[6,8,4,128]{3,2,1,0:T(4,128)} %get-tuple-element.9), channel_id=1, source_target_pairs={{1,0},{2,1},{3,2},{4,3},{5,4},{6,5},{7,6},{9,8},{10,9},{11,10},{12... | collective-permute-start | bytes 294920 | tf_op jit(solution)/shard_map/ppermute | solution.py:21
  25.2 17.1 %collective-permute-done.2 = f32[6,8,4,128]{3,2,1,0:T(4,128)S(1)} collective-permute-done((f32[6,8,4,128]{3,2,1,0:T(4,128)}, f32[6,8,4,128]{3,2,1,0:T(4,128)S(1)}, u32[]{:S(2)}, u32[]{:S(2)}) %collective-permute-start.2) | collective-permute-done | bytes 98336 | tf_op jit(solution)/shard_map/ppermute | solution.py:21
  42.3 0.0 collective-permute-done.3
  42.3 15.1 %collective-permute-start.5 = (f32[2,6,4,4,128]{4,3,2,1,0:T(4,128)S(1)}, f32[2,6,4,4,128]{4,3,2,1,0:T(4,128)S(1)}, u32[]{:S(2)}, u32[]{:S(2)}) collective-permute-start(f32[2,6,4,4,128]{4,3,2,1,0:T(4,128)S(1)} %get-tuple-element.10), channel_id=1, source_target_pairs={{0,504},{8,0},{16,8},{24,16},{32,24},{40,32},{48,40},{56,48},{64,5... | collective-permute-start | bytes 294920 | tf_op jit(solution)/shard_map/ppermute | solution.py:21
  57.5 1.9 %collective-permute-start.4 = (f32[2,6,4,4,128]{4,3,2,1,0:T(4,128)S(1)}, f32[2,6,4,4,128]{4,3,2,1,0:T(4,128)S(1)}, u32[]{:S(2)}, u32[]{:S(2)}) collective-permute-start(f32[2,6,4,4,128]{4,3,2,1,0:T(4,128)S(1)} %get-tuple-element.11), channel_id=1, source_target_pairs={{0,8},{8,16},{16,24},{24,32},{32,40},{40,48},{48,56},{56,64},{64,7... | collective-permute-start | bytes 294920 | tf_op jit(solution)/shard_map/ppermute | solution.py:21
  59.4 0.7 pad_maximum_fusion.lat_own
  60.1 0.0 collective-permute-done.5.corner_e
  60.1 0.0 copy-start.2
  60.1 7.5 %collective-permute-done.4.corner_w = f32[2,6,4,4,128]{4,3,2,1,0:T(4,128)S(1)} collective-permute-done((f32[2,6,4,4,128]{4,3,2,1,0:T(4,128)S(1)}, f32[2,6,4,4,128]{4,3,2,1,0:T(4,128)S(1)}, u32[]{:S(2)}, u32[]{:S(2)}) %collective-permute-start.4) | collective-permute-done | bytes 98336 | tf_op jit(solution)/shard_map/ppermute | solution.py:21
  67.6 0.0 copy-start.3
  67.6 0.0 collective-permute-done.1.east_p
  67.6 0.0 copy-start.1
  67.6 0.0 collective-permute-done.west_p
  67.6 0.0 copy-start
  67.6 0.0 copy-done.2
  67.7 0.6 copy-done.3
  68.3 0.4 copy-done.1
  68.7 0.4 copy-done
  69.1 14.8 %shard_map.60 = (f32[8,224,128]{2,1,0:T(8,128)}, f32[8,224,128]{2,1,0:T(8,128)}) custom-call(f32[8,224,128]{2,1,0:T(8,128)} %conc_in.1, bf16[3,8,224,128]{3,2,1,0:T(8,128)(2,1)} %wind_in.1, bf16[8,224,128]{2,1,0:T(8,128)(2,1)} %kappa_in.1, bf16[8,224,128]{2,1,0:T(8,128)(2,1)} %obs_in.1, bf16[23,224,128]{2,1,0:T(8,128)(2,1)} %copy-done, ...), custom_call_target="tpu_custom_call" | custom-call | tf_op jit(solution)/shard_map/pallas_call | solution.py:221
  (1 shorter events, 0.0 us)
Async XLA Ops:
  4.1 63.5 %collective-permute-start = (bf16[23,224,128]{2,1,0:T(8,128)(2,1)}, bf16[23,224,128]{2,1,0:T(8,128)(2,1)S(1)}, u32[]{:S(2)}, u32[]{:S(2)}) collective-permute-start(bf16[23,224,128]{2,1,0:T(8,128)(2,1)} %get-tuple-element.6), channel_id=1, source_target_pairs={{0,8},{8,16},{16,24},{24,32},{32,40},{40,48},{48,56},{56,64},{64,7... | collective-permute-start | bytes 3956744 | tf_op jit(solution)/shard_map/ppermute | solution.py:21
  6.0 61.6 %collective-permute-start.1 = (bf16[21,224,128]{2,1,0:T(8,128)(2,1)}, bf16[21,224,128]{2,1,0:T(8,128)(2,1)S(1)}, u32[]{:S(2)}, u32[]{:S(2)}) collective-permute-start(bf16[21,224,128]{2,1,0:T(8,128)(2,1)} %get-tuple-element.7), channel_id=1, source_target_pairs={{0,504},{8,0},{16,8},{24,16},{32,24},{40,32},{48,40},{56,48},{64,5... | collective-permute-start | bytes 3612680 | tf_op jit(solution)/shard_map/ppermute | solution.py:21
  19.3 23.0 %collective-permute-start.2 = (f32[6,8,4,128]{3,2,1,0:T(4,128)}, f32[6,8,4,128]{3,2,1,0:T(4,128)S(1)}, u32[]{:S(2)}, u32[]{:S(2)}) collective-permute-start(f32[6,8,4,128]{3,2,1,0:T(4,128)} %get-tuple-element.8), channel_id=1, source_target_pairs={{0,1},{1,2},{2,3},{3,4},{4,5},{5,6},{6,7},{8,9},{9,10},{10,11},{11... | collective-permute-start | bytes 294920 | tf_op jit(solution)/shard_map/ppermute | solution.py:21
  22.6 19.7 %collective-permute-start.3 = (f32[6,8,4,128]{3,2,1,0:T(4,128)}, f32[6,8,4,128]{3,2,1,0:T(4,128)S(1)}, u32[]{:S(2)}, u32[]{:S(2)}) collective-permute-start(f32[6,8,4,128]{3,2,1,0:T(4,128)} %get-tuple-element.9), channel_id=1, source_target_pairs={{1,0},{2,1},{3,2},{4,3},{5,4},{6,5},{7,6},{9,8},{10,9},{11,10},{12... | collective-permute-start | bytes 294920 | tf_op jit(solution)/shard_map/ppermute | solution.py:21
  42.3 17.8 %collective-permute-start.5 = (f32[2,6,4,4,128]{4,3,2,1,0:T(4,128)S(1)}, f32[2,6,4,4,128]{4,3,2,1,0:T(4,128)S(1)}, u32[]{:S(2)}, u32[]{:S(2)}) collective-permute-start(f32[2,6,4,4,128]{4,3,2,1,0:T(4,128)S(1)} %get-tuple-element.10), channel_id=1, source_target_pairs={{0,504},{8,0},{16,8},{24,16},{32,24},{40,32},{48,40},{56,48},{64,5... | collective-permute-start | bytes 294920 | tf_op jit(solution)/shard_map/ppermute | solution.py:21
  57.5 10.2 %collective-permute-start.4 = (f32[2,6,4,4,128]{4,3,2,1,0:T(4,128)S(1)}, f32[2,6,4,4,128]{4,3,2,1,0:T(4,128)S(1)}, u32[]{:S(2)}, u32[]{:S(2)}) collective-permute-start(f32[2,6,4,4,128]{4,3,2,1,0:T(4,128)S(1)} %get-tuple-element.11), channel_id=1, source_target_pairs={{0,8},{8,16},{16,24},{24,32},{32,40},{40,48},{48,56},{56,64},{64,7... | collective-permute-start | bytes 294920 | tf_op jit(solution)/shard_map/ppermute | solution.py:21
  60.1 7.5 %copy-start.2 = (f32[2,6,4,4,128]{4,3,2,1,0:T(4,128)}, f32[2,6,4,4,128]{4,3,2,1,0:T(4,128)S(1)}, u32[]{:S(2)}) copy-start(f32[2,6,4,4,128]{4,3,2,1,0:T(4,128)S(1)} %collective-permute-done.5.corner_e) | copy-start | bytes 294916
  67.6 0.6 copy-start.3
  67.6 1.1 %copy-start.1 = (bf16[21,224,128]{2,1,0:T(8,128)(2,1)}, bf16[21,224,128]{2,1,0:T(8,128)(2,1)S(1)}, u32[]{:S(2)}) copy-start(bf16[21,224,128]{2,1,0:T(8,128)(2,1)S(1)} %collective-permute-done.1.east_p) | copy-start | bytes 3612676
  67.6 1.5 %copy-start = (bf16[23,224,128]{2,1,0:T(8,128)(2,1)}, bf16[23,224,128]{2,1,0:T(8,128)(2,1)S(1)}, u32[]{:S(2)}) copy-start(bf16[23,224,128]{2,1,0:T(8,128)(2,1)S(1)} %collective-permute-done.west_p) | copy-start | bytes 3956740

commit v4 on v3

--- a/solution.py
+++ b/solution.py
@@ -126,7 +126,7 @@
             oth_ref[d, i] = oth
         return carry
 
-    lax.fori_loop(0, rows, coef_row, 0)
+    lax.fori_loop(0, rows, coef_row, 0, unroll=2)
 
     def flux0(src, i):
         return own_ref[0, i] * src[i] + oth_ref[0, i] * src[i + 1]
@@ -143,7 +143,7 @@
             dst[i] = out
             return f0
 
-        lax.fori_loop(lo, hi, row, flux0(src, lo - 1))
+        lax.fori_loop(lo, hi, row, flux0(src, lo - 1), unroll=2)
 
     def part0(src, i):
         return oth_ref[0, i] * (src[i + 1] - src[i])
@@ -176,7 +176,7 @@
         lam1_ref[i] = out
         return p0
 
-    lax.fori_loop(3, rows - 3, lam1_row, part0(lam2_ref, 2))
+    lax.fori_loop(3, rows - 3, lam1_row, part0(lam2_ref, 2), unroll=2)
 
     def last_row(i, west0):
         out, p0, gaps1 = retreat_row(lam1_ref, i, west0)
@@ -187,7 +187,7 @@
         gk_ref[i - h] = kappa[PAD:lats - PAD]
         return p0
 
-    lax.fori_loop(h, rows - h, last_row, part0(lam1_ref, h - 1))
+    lax.fori_loop(h, rows - h, last_row, part0(lam1_ref, h - 1), unroll=2)
 
 
 def chain(concentration, wind, kappa, observed):

time: 84.2 us -> 82.1 us (0.975)
  Pallas kernels: 18.3 us -> 16.2 us
    pallas_call x1, Pallas kernels: 14.8 us -> 12.8 us  [chain(): pl.pallas_call(functools.partial(stencil_kernel, west_rows, east_rows, la...]
where the time goes in v4:
time: 82.1 us; the launch traced here: 81.9 us
  starting transfers between devices  38.1 us (46%)
  waiting for transfers between devices  24.6 us (30%)
  Pallas kernels  16.2 us (20%)
  local copies, waits for them, and re-layouts  1.47 us (2%)
    ppermute x6, starting transfers between devices, passed_along(): return lax.ppermute(value, axis, pairs)  38.1 us
    ppermute x6, waiting for transfers between devices, passed_along(): return lax.ppermute(value, axis, pairs)  24.6 us
    pallas_call x1, Pallas kernels, chain(): pl.pallas_call(functools.partial(stencil_kernel, west_rows, east_rows, la...  12.8 us
    pallas_call x1, Pallas kernels, chain(): pl.pallas_call(functools.partial(pack_kernel, west_rows, east_rows), out_...  3.46 us
  transfers between devices with their start and end apart: 6, of which 2 were waited for; matrix products, arithmetic and copies ran while one was open for 1% of the time, Pallas kernels for 0%

profile of v4, /device:TPU:6, one launch (start us, length us, event | category | flops | bytes accessed | tf_op | source)
XLA Modules:
  0.0 81.9 jit_solution(17079250205278353247)
XLA Ops:
  0.6 3.5 %shard_map.59 = (bf16[21,224,128]{2,1,0:T(8,128)(2,1)}, bf16[23,224,128]{2,1,0:T(8,128)(2,1)}, f32[6,8,4,128]{3,2,1,0:T(4,128)}, f32[6,8,4,128]{3,2,1,0:T(4,128)}) custom-call(f32[8,224,128]{2,1,0:T(8,128)} %conc_in.1, bf16[3,8,224,128]{3,2,1,0:T(8,128)(2,1)} %wind_in.1, bf16[8,224,128]{2,1,0:T(8,128)(2,1)} %kappa_in.1, bf16[8,224,128]{2,1,0:T(8,128)(2,1)} %obs_in.1), custom_call_target="tpu_custom_call" | custom-call | tf_op jit(solution)/shard_map/pallas_call | solution.py:202
  4.1 1.9 %collective-permute-start = (bf16[23,224,128]{2,1,0:T(8,128)(2,1)}, bf16[23,224,128]{2,1,0:T(8,128)(2,1)S(1)}, u32[]{:S(2)}, u32[]{:S(2)}) collective-permute-start(bf16[23,224,128]{2,1,0:T(8,128)(2,1)} %get-tuple-element.6), channel_id=1, source_target_pairs={{0,8},{8,16},{16,24},{24,32},{32,40},{40,48},{48,56},{56,64},{64,7... | collective-permute-start | bytes 3956744 | tf_op jit(solution)/shard_map/ppermute | solution.py:21
  6.0 13.3 %collective-permute-start.1 = (bf16[21,224,128]{2,1,0:T(8,128)(2,1)}, bf16[21,224,128]{2,1,0:T(8,128)(2,1)S(1)}, u32[]{:S(2)}, u32[]{:S(2)}) collective-permute-start(bf16[21,224,128]{2,1,0:T(8,128)(2,1)} %get-tuple-element.7), channel_id=1, source_target_pairs={{0,504},{8,0},{16,8},{24,16},{32,24},{40,32},{48,40},{56,48},{64,5... | collective-permute-start | bytes 3612680 | tf_op jit(solution)/shard_map/ppermute | solution.py:21
  19.3 3.3 %collective-permute-start.2 = (f32[6,8,4,128]{3,2,1,0:T(4,128)}, f32[6,8,4,128]{3,2,1,0:T(4,128)S(1)}, u32[]{:S(2)}, u32[]{:S(2)}) collective-permute-start(f32[6,8,4,128]{3,2,1,0:T(4,128)} %get-tuple-element.8), channel_id=1, source_target_pairs={{0,1},{1,2},{2,3},{3,4},{4,5},{5,6},{6,7},{8,9},{9,10},{10,11},{11... | collective-permute-start | bytes 294920 | tf_op jit(solution)/shard_map/ppermute | solution.py:21
  22.6 2.5 %collective-permute-start.3 = (f32[6,8,4,128]{3,2,1,0:T(4,128)}, f32[6,8,4,128]{3,2,1,0:T(4,128)S(1)}, u32[]{:S(2)}, u32[]{:S(2)}) collective-permute-start(f32[6,8,4,128]{3,2,1,0:T(4,128)} %get-tuple-element.9), channel_id=1, source_target_pairs={{1,0},{2,1},{3,2},{4,3},{5,4},{6,5},{7,6},{9,8},{10,9},{11,10},{12... | collective-permute-start | bytes 294920 | tf_op jit(solution)/shard_map/ppermute | solution.py:21
  25.2 17.1 %collective-permute-done.2 = f32[6,8,4,128]{3,2,1,0:T(4,128)S(1)} collective-permute-done((f32[6,8,4,128]{3,2,1,0:T(4,128)}, f32[6,8,4,128]{3,2,1,0:T(4,128)S(1)}, u32[]{:S(2)}, u32[]{:S(2)}) %collective-permute-start.2) | collective-permute-done | bytes 98336 | tf_op jit(solution)/shard_map/ppermute | solution.py:21
  42.3 0.0 collective-permute-done.3
  42.3 15.1 %collective-permute-start.5 = (f32[2,6,4,4,128]{4,3,2,1,0:T(4,128)S(1)}, f32[2,6,4,4,128]{4,3,2,1,0:T(4,128)S(1)}, u32[]{:S(2)}, u32[]{:S(2)}) collective-permute-start(f32[2,6,4,4,128]{4,3,2,1,0:T(4,128)S(1)} %get-tuple-element.10), channel_id=1, source_target_pairs={{0,504},{8,0},{16,8},{24,16},{32,24},{40,32},{48,40},{56,48},{64,5... | collective-permute-start | bytes 294920 | tf_op jit(solution)/shard_map/ppermute | solution.py:21
  57.5 1.9 %collective-permute-start.4 = (f32[2,6,4,4,128]{4,3,2,1,0:T(4,128)S(1)}, f32[2,6,4,4,128]{4,3,2,1,0:T(4,128)S(1)}, u32[]{:S(2)}, u32[]{:S(2)}) collective-permute-start(f32[2,6,4,4,128]{4,3,2,1,0:T(4,128)S(1)} %get-tuple-element.11), channel_id=1, source_target_pairs={{0,8},{8,16},{16,24},{24,32},{32,40},{40,48},{48,56},{56,64},{64,7... | collective-permute-start | bytes 294920 | tf_op jit(solution)/shard_map/ppermute | solution.py:21
  59.4 0.7 pad_maximum_fusion.lat_own
  60.1 0.0 collective-permute-done.5.corner_e
  60.1 0.0 copy-start.2
  60.1 7.5 %collective-permute-done.4.corner_w = f32[2,6,4,4,128]{4,3,2,1,0:T(4,128)S(1)} collective-permute-done((f32[2,6,4,4,128]{4,3,2,1,0:T(4,128)S(1)}, f32[2,6,4,4,128]{4,3,2,1,0:T(4,128)S(1)}, u32[]{:S(2)}, u32[]{:S(2)}) %collective-permute-start.4) | collective-permute-done | bytes 98336 | tf_op jit(solution)/shard_map/ppermute | solution.py:21
  67.6 0.0 copy-start.3
  67.6 0.0 collective-permute-done.1.east_p
  67.6 0.0 copy-start.1
  67.6 0.0 collective-permute-done.west_p
  67.6 0.0 copy-start
  67.6 0.0 copy-done.2
  67.7 0.6 copy-done.3
  68.3 0.4 copy-done.1
  68.7 0.4 copy-done
  69.1 12.8 %shard_map.60 = (f32[8,224,128]{2,1,0:T(8,128)}, f32[8,224,128]{2,1,0:T(8,128)}) custom-call(f32[8,224,128]{2,1,0:T(8,128)} %conc_in.1, bf16[3,8,224,128]{3,2,1,0:T(8,128)(2,1)} %wind_in.1, bf16[8,224,128]{2,1,0:T(8,128)(2,1)} %kappa_in.1, bf16[8,224,128]{2,1,0:T(8,128)(2,1)} %obs_in.1, bf16[23,224,128]{2,1,0:T(8,128)(2,1)} %copy-done, ...), custom_call_target="tpu_custom_call" | custom-call | tf_op jit(solution)/shard_map/pallas_call | solution.py:221
  (1 shorter events, 0.0 us)
Async XLA Ops:
  4.1 63.5 %collective-permute-start = (bf16[23,224,128]{2,1,0:T(8,128)(2,1)}, bf16[23,224,128]{2,1,0:T(8,128)(2,1)S(1)}, u32[]{:S(2)}, u32[]{:S(2)}) collective-permute-start(bf16[23,224,128]{2,1,0:T(8,128)(2,1)} %get-tuple-element.6), channel_id=1, source_target_pairs={{0,8},{8,16},{16,24},{24,32},{32,40},{40,48},{48,56},{56,64},{64,7... | collective-permute-start | bytes 3956744 | tf_op jit(solution)/shard_map/ppermute | solution.py:21
  6.0 61.6 %collective-permute-start.1 = (bf16[21,224,128]{2,1,0:T(8,128)(2,1)}, bf16[21,224,128]{2,1,0:T(8,128)(2,1)S(1)}, u32[]{:S(2)}, u32[]{:S(2)}) collective-permute-start(bf16[21,224,128]{2,1,0:T(8,128)(2,1)} %get-tuple-element.7), channel_id=1, source_target_pairs={{0,504},{8,0},{16,8},{24,16},{32,24},{40,32},{48,40},{56,48},{64,5... | collective-permute-start | bytes 3612680 | tf_op jit(solution)/shard_map/ppermute | solution.py:21
  19.3 23.0 %collective-permute-start.2 = (f32[6,8,4,128]{3,2,1,0:T(4,128)}, f32[6,8,4,128]{3,2,1,0:T(4,128)S(1)}, u32[]{:S(2)}, u32[]{:S(2)}) collective-permute-start(f32[6,8,4,128]{3,2,1,0:T(4,128)} %get-tuple-element.8), channel_id=1, source_target_pairs={{0,1},{1,2},{2,3},{3,4},{4,5},{5,6},{6,7},{8,9},{9,10},{10,11},{11... | collective-permute-start | bytes 294920 | tf_op jit(solution)/shard_map/ppermute | solution.py:21
  22.6 19.7 %collective-permute-start.3 = (f32[6,8,4,128]{3,2,1,0:T(4,128)}, f32[6,8,4,128]{3,2,1,0:T(4,128)S(1)}, u32[]{:S(2)}, u32[]{:S(2)}) collective-permute-start(f32[6,8,4,128]{3,2,1,0:T(4,128)} %get-tuple-element.9), channel_id=1, source_target_pairs={{1,0},{2,1},{3,2},{4,3},{5,4},{6,5},{7,6},{9,8},{10,9},{11,10},{12... | collective-permute-start | bytes 294920 | tf_op jit(solution)/shard_map/ppermute | solution.py:21
  42.3 17.8 %collective-permute-start.5 = (f32[2,6,4,4,128]{4,3,2,1,0:T(4,128)S(1)}, f32[2,6,4,4,128]{4,3,2,1,0:T(4,128)S(1)}, u32[]{:S(2)}, u32[]{:S(2)}) collective-permute-start(f32[2,6,4,4,128]{4,3,2,1,0:T(4,128)S(1)} %get-tuple-element.10), channel_id=1, source_target_pairs={{0,504},{8,0},{16,8},{24,16},{32,24},{40,32},{48,40},{56,48},{64,5... | collective-permute-start | bytes 294920 | tf_op jit(solution)/shard_map/ppermute | solution.py:21
  57.5 10.2 %collective-permute-start.4 = (f32[2,6,4,4,128]{4,3,2,1,0:T(4,128)S(1)}, f32[2,6,4,4,128]{4,3,2,1,0:T(4,128)S(1)}, u32[]{:S(2)}, u32[]{:S(2)}) collective-permute-start(f32[2,6,4,4,128]{4,3,2,1,0:T(4,128)S(1)} %get-tuple-element.11), channel_id=1, source_target_pairs={{0,8},{8,16},{16,24},{24,32},{32,40},{40,48},{48,56},{56,64},{64,7... | collective-permute-start | bytes 294920 | tf_op jit(solution)/shard_map/ppermute | solution.py:21
  60.1 7.5 %copy-start.2 = (f32[2,6,4,4,128]{4,3,2,1,0:T(4,128)}, f32[2,6,4,4,128]{4,3,2,1,0:T(4,128)S(1)}, u32[]{:S(2)}) copy-start(f32[2,6,4,4,128]{4,3,2,1,0:T(4,128)S(1)} %collective-permute-done.5.corner_e) | copy-start | bytes 294916
  67.6 0.6 copy-start.3
  67.6 1.1 %copy-start.1 = (bf16[21,224,128]{2,1,0:T(8,128)(2,1)}, bf16[21,224,128]{2,1,0:T(8,128)(2,1)S(1)}, u32[]{:S(2)}) copy-start(bf16[21,224,128]{2,1,0:T(8,128)(2,1)S(1)} %collective-permute-done.1.east_p) | copy-start | bytes 3612676
  67.6 1.5 %copy-start = (bf16[23,224,128]{2,1,0:T(8,128)(2,1)}, bf16[23,224,128]{2,1,0:T(8,128)(2,1)S(1)}, u32[]{:S(2)}) copy-start(bf16[23,224,128]{2,1,0:T(8,128)(2,1)S(1)} %collective-permute-done.west_p) | copy-start | bytes 3956740

commit v5 on v4

--- a/solution.py
+++ b/solution.py
@@ -126,7 +126,7 @@
             oth_ref[d, i] = oth
         return carry
 
-    lax.fori_loop(0, rows, coef_row, 0, unroll=2)
+    lax.fori_loop(0, rows, coef_row, 0, unroll=4)
 
     def flux0(src, i):
         return own_ref[0, i] * src[i] + oth_ref[0, i] * src[i + 1]
@@ -143,7 +143,7 @@
             dst[i] = out
             return f0
 
-        lax.fori_loop(lo, hi, row, flux0(src, lo - 1), unroll=2)
+        lax.fori_loop(lo, hi, row, flux0(src, lo - 1), unroll=4)
 
     def part0(src, i):
         return oth_ref[0, i] * (src[i + 1] - src[i])
@@ -176,7 +176,7 @@
         lam1_ref[i] = out
         return p0
 
-    lax.fori_loop(3, rows - 3, lam1_row, part0(lam2_ref, 2), unroll=2)
+    lax.fori_loop(3, rows - 3, lam1_row, part0(lam2_ref, 2), unroll=4)
 
     def last_row(i, west0):
         out, p0, gaps1 = retreat_row(lam1_ref, i, west0)
@@ -187,7 +187,7 @@
         gk_ref[i - h] = kappa[PAD:lats - PAD]
         return p0
 
-    lax.fori_loop(h, rows - h, last_row, part0(lam1_ref, h - 1), unroll=2)
+    lax.fori_loop(h, rows - h, last_row, part0(lam1_ref, h - 1), unroll=4)
 
 
 def chain(concentration, wind, kappa, observed):

time: 82.1 us -> 82 us (level)
  no operation moved by 1% of the time
where the time goes in v5:
time: 82 us; the launch traced here: 81.7 us
  starting transfers between devices  38.1 us (46%)
  waiting for transfers between devices  24.6 us (30%)
  Pallas kernels  16.1 us (20%)
  local copies, waits for them, and re-layouts  1.47 us (2%)
    ppermute x6, starting transfers between devices, passed_along(): return lax.ppermute(value, axis, pairs)  38.1 us
    ppermute x6, waiting for transfers between devices, passed_along(): return lax.ppermute(value, axis, pairs)  24.6 us
    pallas_call x1, Pallas kernels, chain(): pl.pallas_call(functools.partial(stencil_kernel, west_rows, east_rows, la...  12.6 us
    pallas_call x1, Pallas kernels, chain(): pl.pallas_call(functools.partial(pack_kernel, west_rows, east_rows), out_...  3.46 us
  transfers between devices with their start and end apart: 6, of which 2 were waited for; matrix products, arithmetic and copies ran while one was open for 1% of the time, Pallas kernels for 0%

profile of v5, /device:TPU:6, one launch (start us, length us, event | category | flops | bytes accessed | tf_op | source)
XLA Modules:
  0.0 81.7 jit_solution(13179212164616548329)
XLA Ops:
  0.6 3.5 %shard_map.59 = (bf16[21,224,128]{2,1,0:T(8,128)(2,1)}, bf16[23,224,128]{2,1,0:T(8,128)(2,1)}, f32[6,8,4,128]{3,2,1,0:T(4,128)}, f32[6,8,4,128]{3,2,1,0:T(4,128)}) custom-call(f32[8,224,128]{2,1,0:T(8,128)} %conc_in.1, bf16[3,8,224,128]{3,2,1,0:T(8,128)(2,1)} %wind_in.1, bf16[8,224,128]{2,1,0:T(8,128)(2,1)} %kappa_in.1, bf16[8,224,128]{2,1,0:T(8,128)(2,1)} %obs_in.1), custom_call_target="tpu_custom_call" | custom-call | tf_op jit(solution)/shard_map/pallas_call | solution.py:202
  4.1 1.9 %collective-permute-start = (bf16[23,224,128]{2,1,0:T(8,128)(2,1)}, bf16[23,224,128]{2,1,0:T(8,128)(2,1)S(1)}, u32[]{:S(2)}, u32[]{:S(2)}) collective-permute-start(bf16[23,224,128]{2,1,0:T(8,128)(2,1)} %get-tuple-element.6), channel_id=1, source_target_pairs={{0,8},{8,16},{16,24},{24,32},{32,40},{40,48},{48,56},{56,64},{64,7... | collective-permute-start | bytes 3956744 | tf_op jit(solution)/shard_map/ppermute | solution.py:21
  6.0 13.3 %collective-permute-start.1 = (bf16[21,224,128]{2,1,0:T(8,128)(2,1)}, bf16[21,224,128]{2,1,0:T(8,128)(2,1)S(1)}, u32[]{:S(2)}, u32[]{:S(2)}) collective-permute-start(bf16[21,224,128]{2,1,0:T(8,128)(2,1)} %get-tuple-element.7), channel_id=1, source_target_pairs={{0,504},{8,0},{16,8},{24,16},{32,24},{40,32},{48,40},{56,48},{64,5... | collective-permute-start | bytes 3612680 | tf_op jit(solution)/shard_map/ppermute | solution.py:21
  19.3 3.3 %collective-permute-start.2 = (f32[6,8,4,128]{3,2,1,0:T(4,128)}, f32[6,8,4,128]{3,2,1,0:T(4,128)S(1)}, u32[]{:S(2)}, u32[]{:S(2)}) collective-permute-start(f32[6,8,4,128]{3,2,1,0:T(4,128)} %get-tuple-element.8), channel_id=1, source_target_pairs={{0,1},{1,2},{2,3},{3,4},{4,5},{5,6},{6,7},{8,9},{9,10},{10,11},{11... | collective-permute-start | bytes 294920 | tf_op jit(solution)/shard_map/ppermute | solution.py:21
  22.6 2.5 %collective-permute-start.3 = (f32[6,8,4,128]{3,2,1,0:T(4,128)}, f32[6,8,4,128]{3,2,1,0:T(4,128)S(1)}, u32[]{:S(2)}, u32[]{:S(2)}) collective-permute-start(f32[6,8,4,128]{3,2,1,0:T(4,128)} %get-tuple-element.9), channel_id=1, source_target_pairs={{1,0},{2,1},{3,2},{4,3},{5,4},{6,5},{7,6},{9,8},{10,9},{11,10},{12... | collective-permute-start | bytes 294920 | tf_op jit(solution)/shard_map/ppermute | solution.py:21
  25.2 17.1 %collective-permute-done.2 = f32[6,8,4,128]{3,2,1,0:T(4,128)S(1)} collective-permute-done((f32[6,8,4,128]{3,2,1,0:T(4,128)}, f32[6,8,4,128]{3,2,1,0:T(4,128)S(1)}, u32[]{:S(2)}, u32[]{:S(2)}) %collective-permute-start.2) | collective-permute-done | bytes 98336 | tf_op jit(solution)/shard_map/ppermute | solution.py:21
  42.3 0.0 collective-permute-done.3
  42.3 15.1 %collective-permute-start.5 = (f32[2,6,4,4,128]{4,3,2,1,0:T(4,128)S(1)}, f32[2,6,4,4,128]{4,3,2,1,0:T(4,128)S(1)}, u32[]{:S(2)}, u32[]{:S(2)}) collective-permute-start(f32[2,6,4,4,128]{4,3,2,1,0:T(4,128)S(1)} %get-tuple-element.10), channel_id=1, source_target_pairs={{0,504},{8,0},{16,8},{24,16},{32,24},{40,32},{48,40},{56,48},{64,5... | collective-permute-start | bytes 294920 | tf_op jit(solution)/shard_map/ppermute | solution.py:21
  57.5 1.9 %collective-permute-start.4 = (f32[2,6,4,4,128]{4,3,2,1,0:T(4,128)S(1)}, f32[2,6,4,4,128]{4,3,2,1,0:T(4,128)S(1)}, u32[]{:S(2)}, u32[]{:S(2)}) collective-permute-start(f32[2,6,4,4,128]{4,3,2,1,0:T(4,128)S(1)} %get-tuple-element.11), channel_id=1, source_target_pairs={{0,8},{8,16},{16,24},{24,32},{32,40},{40,48},{48,56},{56,64},{64,7... | collective-permute-start | bytes 294920 | tf_op jit(solution)/shard_map/ppermute | solution.py:21
  59.4 0.7 pad_maximum_fusion.lat_own
  60.1 0.0 collective-permute-done.5.corner_e
  60.1 0.0 copy-start.2
  60.1 7.5 %collective-permute-done.4.corner_w = f32[2,6,4,4,128]{4,3,2,1,0:T(4,128)S(1)} collective-permute-done((f32[2,6,4,4,128]{4,3,2,1,0:T(4,128)S(1)}, f32[2,6,4,4,128]{4,3,2,1,0:T(4,128)S(1)}, u32[]{:S(2)}, u32[]{:S(2)}) %collective-permute-start.4) | collective-permute-done | bytes 98336 | tf_op jit(solution)/shard_map/ppermute | solution.py:21
  67.6 0.0 copy-start.3
  67.6 0.0 collective-permute-done.1.east_p
  67.6 0.0 copy-start.1
  67.6 0.0 collective-permute-done.west_p
  67.6 0.0 copy-start
  67.6 0.0 copy-done.2
  67.7 0.6 copy-done.3
  68.3 0.4 copy-done.1
  68.7 0.4 copy-done
  69.1 12.6 %shard_map.60 = (f32[8,224,128]{2,1,0:T(8,128)}, f32[8,224,128]{2,1,0:T(8,128)}) custom-call(f32[8,224,128]{2,1,0:T(8,128)} %conc_in.1, bf16[3,8,224,128]{3,2,1,0:T(8,128)(2,1)} %wind_in.1, bf16[8,224,128]{2,1,0:T(8,128)(2,1)} %kappa_in.1, bf16[8,224,128]{2,1,0:T(8,128)(2,1)} %obs_in.1, bf16[23,224,128]{2,1,0:T(8,128)(2,1)} %copy-done, ...), custom_call_target="tpu_custom_call" | custom-call | tf_op jit(solution)/shard_map/pallas_call | solution.py:221
  (1 shorter events, 0.0 us)
Async XLA Ops:
  4.1 63.5 %collective-permute-start = (bf16[23,224,128]{2,1,0:T(8,128)(2,1)}, bf16[23,224,128]{2,1,0:T(8,128)(2,1)S(1)}, u32[]{:S(2)}, u32[]{:S(2)}) collective-permute-start(bf16[23,224,128]{2,1,0:T(8,128)(2,1)} %get-tuple-element.6), channel_id=1, source_target_pairs={{0,8},{8,16},{16,24},{24,32},{32,40},{40,48},{48,56},{56,64},{64,7... | collective-permute-start | bytes 3956744 | tf_op jit(solution)/shard_map/ppermute | solution.py:21
  6.0 61.6 %collective-permute-start.1 = (bf16[21,224,128]{2,1,0:T(8,128)(2,1)}, bf16[21,224,128]{2,1,0:T(8,128)(2,1)S(1)}, u32[]{:S(2)}, u32[]{:S(2)}) collective-permute-start(bf16[21,224,128]{2,1,0:T(8,128)(2,1)} %get-tuple-element.7), channel_id=1, source_target_pairs={{0,504},{8,0},{16,8},{24,16},{32,24},{40,32},{48,40},{56,48},{64,5... | collective-permute-start | bytes 3612680 | tf_op jit(solution)/shard_map/ppermute | solution.py:21
  19.3 23.0 %collective-permute-start.2 = (f32[6,8,4,128]{3,2,1,0:T(4,128)}, f32[6,8,4,128]{3,2,1,0:T(4,128)S(1)}, u32[]{:S(2)}, u32[]{:S(2)}) collective-permute-start(f32[6,8,4,128]{3,2,1,0:T(4,128)} %get-tuple-element.8), channel_id=1, source_target_pairs={{0,1},{1,2},{2,3},{3,4},{4,5},{5,6},{6,7},{8,9},{9,10},{10,11},{11... | collective-permute-start | bytes 294920 | tf_op jit(solution)/shard_map/ppermute | solution.py:21
  22.6 19.7 %collective-permute-start.3 = (f32[6,8,4,128]{3,2,1,0:T(4,128)}, f32[6,8,4,128]{3,2,1,0:T(4,128)S(1)}, u32[]{:S(2)}, u32[]{:S(2)}) collective-permute-start(f32[6,8,4,128]{3,2,1,0:T(4,128)} %get-tuple-element.9), channel_id=1, source_target_pairs={{1,0},{2,1},{3,2},{4,3},{5,4},{6,5},{7,6},{9,8},{10,9},{11,10},{12... | collective-permute-start | bytes 294920 | tf_op jit(solution)/shard_map/ppermute | solution.py:21
  42.3 17.8 %collective-permute-start.5 = (f32[2,6,4,4,128]{4,3,2,1,0:T(4,128)S(1)}, f32[2,6,4,4,128]{4,3,2,1,0:T(4,128)S(1)}, u32[]{:S(2)}, u32[]{:S(2)}) collective-permute-start(f32[2,6,4,4,128]{4,3,2,1,0:T(4,128)S(1)} %get-tuple-element.10), channel_id=1, source_target_pairs={{0,504},{8,0},{16,8},{24,16},{32,24},{40,32},{48,40},{56,48},{64,5... | collective-permute-start | bytes 294920 | tf_op jit(solution)/shard_map/ppermute | solution.py:21
  57.5 10.2 %collective-permute-start.4 = (f32[2,6,4,4,128]{4,3,2,1,0:T(4,128)S(1)}, f32[2,6,4,4,128]{4,3,2,1,0:T(4,128)S(1)}, u32[]{:S(2)}, u32[]{:S(2)}) collective-permute-start(f32[2,6,4,4,128]{4,3,2,1,0:T(4,128)S(1)} %get-tuple-element.11), channel_id=1, source_target_pairs={{0,8},{8,16},{16,24},{24,32},{32,40},{40,48},{48,56},{56,64},{64,7... | collective-permute-start | bytes 294920 | tf_op jit(solution)/shard_map/ppermute | solution.py:21
  60.1 7.5 %copy-start.2 = (f32[2,6,4,4,128]{4,3,2,1,0:T(4,128)}, f32[2,6,4,4,128]{4,3,2,1,0:T(4,128)S(1)}, u32[]{:S(2)}) copy-start(f32[2,6,4,4,128]{4,3,2,1,0:T(4,128)S(1)} %collective-permute-done.5.corner_e) | copy-start | bytes 294916
  67.6 0.6 copy-start.3
  67.6 1.1 %copy-start.1 = (bf16[21,224,128]{2,1,0:T(8,128)(2,1)}, bf16[21,224,128]{2,1,0:T(8,128)(2,1)S(1)}, u32[]{:S(2)}) copy-start(bf16[21,224,128]{2,1,0:T(8,128)(2,1)S(1)} %collective-permute-done.1.east_p) | copy-start | bytes 3612676
  67.6 1.5 %copy-start = (bf16[23,224,128]{2,1,0:T(8,128)(2,1)}, bf16[23,224,128]{2,1,0:T(8,128)(2,1)S(1)}, u32[]{:S(2)}) copy-start(bf16[23,224,128]{2,1,0:T(8,128)(2,1)S(1)} %collective-permute-done.west_p) | copy-start | bytes 3956740
